TPU v7x, 256 devices: a whole 4x4x8 slice. The times are simulated.
256 devices in a mesh: section: 4 (over x), expert: 64 (over y, z, core).
Axes of the slice: x: 4, y: 4, z: 8, core: 2. Of those that a mesh axis runs over, the one named last changes fastest.
Arguments:
- acts: bfloat16 [4, 2, 4096, 3584], P('section', None, 'expert'), may hold values from -6 to 6
- norm_gain: float32 [4, 3584], P('section'), may hold values from 0.1 to 1.9
- router: bfloat16 [4, 3584, 16], P('section'), may hold values from -0.09375 to 0.09375
- routes: int32 [4, 2, 2, 4096, 1], P('section', None, None, 'expert'), may hold values from 0 to 15; in each aligned block of 64 rows (0 to 63, 64 to 127, ..., all dimensions but the last counted through in order) at most 8 rows name the same one
- w_gate: bfloat16 [4, 64, 3584, 256], P('section', 'expert'), may hold values from -0.09375 to 0.09375
- w_up: bfloat16 [4, 64, 3584, 256], P('section', 'expert'), may hold values from -0.09375 to 0.09375
- w_down: bfloat16 [4, 64, 256, 3584], P('section', 'expert'), may hold values from -0.375 to 0.375
Outputs:
- finished: bfloat16 [4, 2, 4096, 3584], P('section', None, 'expert')
Inputs may be any that keep to these rules, and one draw needn't show every extreme that they name: `routes`: within each block of 64 tokens of one device, for each layer, round and micro-batch, no expert is named by more than 8 tokens, a bound that some block reaches.
All inputs are finite; a program needn't handle non-finite values.
Results may differ from a plain program's by a relative error of at most 0.0072.
Values may be sent and summed in bfloat16 or wider, within the bound.
No kernel may reach another device: no remote copies, remote signals or barrier semaphores. Data moves between devices by JAX's collectives and lax.ppermute only.
A program may use at most 128 MiB of HBM per device.

v0:
```python
import jax
import jax.numpy as jnp
from jax import lax
from jax.sharding import Mesh
from jax.sharding import PartitionSpec as P

ROW = ("z", "core")
EXP = ("y", "z", "core")


def passed_along(value, axis, steps):
    count = lax.axis_size(axis)
    pairs = [(source, (source + steps) % count) for source in range(count)]
    return lax.ppermute(value, axis, pairs)


def gathered_blocks(block, axis):
    from_below = passed_along(block, "y", 1)
    from_above = passed_along(block, "y", -1)
    far_low = passed_along(jnp.split(from_below, 2, axis=axis)[0], "y", 1)
    far_high = passed_along(jnp.split(from_above, 2, axis=axis)[1], "y", -1)
    return [block, from_below, from_above, jnp.concatenate([far_low, far_high], axis=axis)]


def body(acts, norm_gain, router, routes, w_gate, w_up, w_down):
    experts_here = router.shape[2]
    row_size = lax.axis_size("z") * lax.axis_size("core")
    tok_local = acts.shape[2]
    width = acts.shape[3]
    capacity = 2 * tok_local // experts_here
    gain_row = norm_gain[0]
    router_mat = router[0]
    gate_mats = gathered_blocks(w_gate[0, 0], 0)
    up_mats = gathered_blocks(w_up[0, 0], 0)
    down_mats = gathered_blocks(w_down[0, 0], 0)
    hid_total = sum(mat.shape[1] for mat in gate_mats)
    gate_up = jnp.concatenate(gate_mats + up_mats, axis=1)
    down_all = jnp.concatenate(down_mats, axis=0)

    def expert_compute(rows_in):
        both = jnp.dot(rows_in, gate_up, preferred_element_type=jnp.float32)
        hidden = (jax.nn.silu(both[:, :hid_total]) * both[:, hid_total:]).astype(jnp.bfloat16)
        return jnp.dot(hidden, down_all, preferred_element_type=jnp.float32).astype(jnp.bfloat16)

    def apply_layer(tokens_in, route_ids):
        x_float = tokens_in.astype(jnp.float32)
        mean_sq = jnp.mean(x_float * x_float, axis=1, keepdims=True)
        normed = (x_float * lax.rsqrt(mean_sq + 1e-06) * gain_row[None, :]).astype(jnp.bfloat16)
        scores = jnp.dot(normed, router_mat, preferred_element_type=jnp.float32)
        chosen = route_ids[:, 0]
        onehot = (chosen[:, None] == jnp.arange(experts_here, dtype=jnp.int32)[None, :]).astype(
            jnp.int32
        )
        gate_val = jax.nn.sigmoid(jnp.sum(scores * onehot.astype(jnp.float32), axis=1))
        slot_of = jnp.sum(jnp.cumsum(onehot, axis=0) * onehot, axis=1) - 1
        flat_slot = chosen * capacity + slot_of
        placing = (
            flat_slot[None, :] == jnp.arange(experts_here * capacity, dtype=jnp.int32)[:, None]
        ).astype(jnp.bfloat16)
        outbox = jnp.dot(placing, normed, preferred_element_type=jnp.float32).astype(jnp.bfloat16)
        outbox = outbox.reshape(row_size, capacity, width)
        arrived = lax.all_to_all(outbox, ROW, split_axis=0, concat_axis=0, tiled=True)
        summed = expert_compute(arrived.reshape(-1, width))
        back = lax.all_to_all(
            summed.reshape(row_size, capacity, width), ROW, split_axis=0, concat_axis=0, tiled=True
        )
        picked = jnp.dot(
            placing.T, back.reshape(experts_here * capacity, width), preferred_element_type=jnp.float32
        )
        return (x_float + gate_val[:, None] * picked).astype(jnp.bfloat16)

    micro_count = acts.shape[1]
    carried = [acts[0, micro_idx] for micro_idx in range(micro_count)]
    for round_idx in range(routes.shape[1]):
        carried = [
            passed_along(apply_layer(carried[micro_idx], routes[0, round_idx, micro_idx]), "section", 1)
            for micro_idx in range(micro_count)
        ]
    return jnp.stack(carried)[None]


def solution(mesh):
    n_sec, n_exp = mesh.devices.shape
    n_core = 2
    n_y = n_exp // (n_core * 8)
    grid = mesh.devices.reshape(n_sec, n_y, n_exp // (n_y * n_core), n_core)
    fine = Mesh(grid, ("section", "y", "z", "core"))
    in_specs = (
        P("section", None, EXP, None),
        P("section", None),
        P("section", None, None),
        P("section", None, None, EXP, None),
        P("section", EXP, None, None),
        P("section", EXP, None, None),
        P("section", EXP, None, None),
    )
    out_specs = P("section", None, EXP, None)
    return jax.shard_map(body, mesh=fine, in_specs=in_specs, out_specs=out_specs, check_vma=False)
```

profile of v0, /device:TPU:1, one launch (start us, length us, event | category | flops | bytes accessed | tf_op | source)
XLA Modules:
  0.0 405.7 jit_solution(457228617594374223)
XLA Ops:
  0.0 2.1 collective-permute-start
  2.1 1.5 collective-permute-start.1
  3.6 2.7 collective-permute-start.5
  8.1 1.4 fusion.24
  11.0 2.4 fusion.4
  13.5 10.1 %all-to-all-start = ((bf16[16,8,3584]{2,1,0:T(8,128)(2,1)}), bf16[16,8,3584]{2,1,0:T(8,128)(2,1)S(1)}, u32[]{:S(2)}, u32[]{:S(2)}) async-start(bf16[16,8,3584]{2,1,0:T(8,128)(2,1)} %fusion.4), calls=%async_computation | async-start | bytes 1835008 | tf_op jit(solution)/shard_map/all_to_all | solution.py:62
  23.6 2.4 fusion.8
  26.0 2.9 constant_dynamic-update-slice_fusion.5
  29.0 12.7 %collective-permute-done = bf16[3584,256]{1,0:T(8,128)(2,1)} collective-permute-done((bf16[3584,256]{1,0:T(8,128)(2,1)}, bf16[3584,256]{1,0:T(8,128)(2,1)}, u32[]{:S(2)}, u32[]{:S(2)}) %collective-permute-start) | collective-permute-done | bytes 1835040 | tf_op jit(solution)/shard_map/ppermute | solution.py:14
  41.7 3.1 collective-permute-start.9
  44.8 1.7 constant_dynamic-update-slice_fusion.10
  49.0 31.9 %collective-permute-done.4 = bf16[3584,256]{1,0:T(8,128)(2,1)S(1)} collective-permute-done((bf16[3584,256]{1,0:T(8,128)(2,1)}, bf16[3584,256]{1,0:T(8,128)(2,1)S(1)}, u32[]{:S(2)}, u32[]{:S(2)}) %collective-permute-start.4) | collective-permute-done | bytes 1835040 | tf_op jit(solution)/shard_map/ppermute | solution.py:14
  80.9 3.2 collective-permute-start.3
  85.5 34.7 %collective-permute-done.8 = bf16[256,3584]{1,0:T(8,128)(2,1)S(1)} collective-permute-done((bf16[256,3584]{1,0:T(8,128)(2,1)}, bf16[256,3584]{1,0:T(8,128)(2,1)S(1)}, u32[]{:S(2)}, u32[]{:S(2)}) %collective-permute-start.8) | collective-permute-done | bytes 1835040 | tf_op jit(solution)/shard_map/ppermute | solution.py:14
  120.2 3.1 collective-permute-start.7
  123.4 3.0 constant_dynamic-update-slice_fusion.4
  126.3 2.9 constant_dynamic-update-slice_fusion.3
  130.5 9.3 %collective-permute-done.2 = bf16[1792,256]{1,0:T(8,128)(2,1)S(1)} collective-permute-done((bf16[1792,256]{1,0:T(8,128)(2,1)S(1)}, bf16[1792,256]{1,0:T(8,128)(2,1)S(1)}, u32[]{:S(2)}, u32[]{:S(2)}) %collective-permute-start.2) | collective-permute-done | bytes 917536 | tf_op jit(solution)/shard_map/ppermute | solution.py:14
  139.9 3.1 collective-permute-start.11
  147.2 2.9 constant_dynamic-update-slice_fusion
  150.1 29.0 %collective-permute-done.10 = bf16[128,3584]{1,0:T(8,128)(2,1)S(1)} collective-permute-done((bf16[128,3584]{1,0:T(8,128)(2,1)S(1)}, bf16[128,3584]{1,0:T(8,128)(2,1)S(1)}, u32[]{:S(2)}, u32[]{:S(2)}) %collective-permute-start.10) | collective-permute-done | bytes 917536 | tf_op jit(solution)/shard_map/ppermute | solution.py:14
  179.3 2.9 copy-done.3
  183.6 11.7 %all-to-all-start.4 = ((bf16[16,8,3584]{2,1,0:T(8,128)(2,1)}), bf16[16,8,3584]{2,1,0:T(8,128)(2,1)S(1)}, u32[]{:S(2)}, u32[]{:S(2)}) async-start(bf16[16,8,3584]{2,1,0:T(8,128)(2,1)} %fusion.8), calls=%async_computation.4 | async-start | bytes 1835008 | tf_op jit(solution)/shard_map/all_to_all | solution.py:62
  195.3 2.2 constant_dynamic-update-slice_fusion.6
  197.4 7.4 %fusion.50 = f32[128,2048]{1,0:T(8,128)S(1)} fusion(bf16[3584,2048]{1,0:T(8,128)(2,1)} %maximum_dynamic-update-slice_fusion, bf16[16,8,3584]{2,1,0:T(8,128)(2,1)S(1)} %all-to-all-done), kind=kOutput, calls=%fused_computation.77 | convolution fusion | flops 1879048192 | bytes 16646144 | tf_op jit(solution)/shard_map/dot_general | solution.py:41
  204.8 2.1 fusion.5
  207.0 13.6 %all-to-all-done.4 = bf16[16,8,3584]{2,1,0:T(8,128)(2,1)S(1)} async-done(((bf16[16,8,3584]{2,1,0:T(8,128)(2,1)}), bf16[16,8,3584]{2,1,0:T(8,128)(2,1)S(1)}, u32[]{:S(2)}, u32[]{:S(2)}) %all-to-all-start.4) | async-done | bytes 917536 | tf_op jit(solution)/shard_map/all_to_all | solution.py:62
  220.6 3.5 all-to-all-start.1
  224.2 7.2 %fusion.44 = f32[128,2048]{1,0:T(8,128)S(1)} fusion(bf16[3584,2048]{1,0:T(8,128)(2,1)} %maximum_dynamic-update-slice_fusion, bf16[16,8,3584]{2,1,0:T(8,128)(2,1)S(1)} %all-to-all-done.4), kind=kOutput, calls=%fused_computation.71 | convolution fusion | flops 1879048192 | bytes 16646144 | tf_op jit(solution)/shard_map/dot_general | solution.py:41
  231.4 5.3 %fusion.9 = bf16[16,8,3584]{2,1,0:T(8,128)(2,1)} fusion(bf16[1024,3584]{1,0:T(8,128)(2,1)} %constant_dynamic-update-slice_fusion.6, f32[128,2048]{1,0:T(8,128)S(1)} %fusion.44), kind=kOutput, calls=%fused_computation.21 | convolution fusion | flops 940769280 | bytes 9306112 | tf_op jit(solution)/shard_map/dot_general | solution.py:43
  236.7 12.5 %all-to-all-done.1 = bf16[16,8,3584]{2,1,0:T(8,128)(2,1)S(1)} async-done(((bf16[16,8,3584]{2,1,0:T(8,128)(2,1)}), bf16[16,8,3584]{2,1,0:T(8,128)(2,1)S(1)}, u32[]{:S(2)}, u32[]{:S(2)}) %all-to-all-start.1) | async-done | bytes 917536 | tf_op jit(solution)/shard_map/all_to_all | solution.py:64
  249.2 3.5 all-to-all-start.5
  254.8 12.3 %collective-permute-done.12 = bf16[64,3584]{1,0:T(8,128)(2,1)S(1)} collective-permute-done((bf16[64,3584]{1,0:T(8,128)(2,1)S(1)}, bf16[64,3584]{1,0:T(8,128)(2,1)S(1)}, u32[]{:S(2)}, u32[]{:S(2)}) %collective-permute-start.12) | collective-permute-done | bytes 458784 | tf_op jit(solution)/shard_map/ppermute | solution.py:14
  268.7 9.2 %all-to-all-done.5 = bf16[16,8,3584]{2,1,0:T(8,128)(2,1)S(1)} async-done(((bf16[16,8,3584]{2,1,0:T(8,128)(2,1)}), bf16[16,8,3584]{2,1,0:T(8,128)(2,1)S(1)}, u32[]{:S(2)}, u32[]{:S(2)}) %all-to-all-start.5) | async-done | bytes 917536 | tf_op jit(solution)/shard_map/all_to_all | solution.py:64
  277.8 3.5 all-to-all-start.2
  283.3 12.2 %collective-permute-done.14 = bf16[64,3584]{1,0:T(8,128)(2,1)S(1)} collective-permute-done((bf16[64,3584]{1,0:T(8,128)(2,1)S(1)}, bf16[64,3584]{1,0:T(8,128)(2,1)S(1)}, u32[]{:S(2)}, u32[]{:S(2)}) %collective-permute-start.14) | collective-permute-done | bytes 458784 | tf_op jit(solution)/shard_map/ppermute | solution.py:14
  297.1 9.3 %all-to-all-done.2 = bf16[16,8,3584]{2,1,0:T(8,128)(2,1)S(1)} async-done(((bf16[16,8,3584]{2,1,0:T(8,128)(2,1)}), bf16[16,8,3584]{2,1,0:T(8,128)(2,1)S(1)}, u32[]{:S(2)}, u32[]{:S(2)}) %all-to-all-start.2) | async-done | bytes 917536 | tf_op jit(solution)/shard_map/all_to_all | solution.py:62
  306.5 3.8 all-to-all-start.6
  310.2 7.2 %fusion.47 = f32[128,2048]{1,0:T(8,128)S(1)} fusion(bf16[3584,2048]{1,0:T(8,128)(2,1)} %maximum_dynamic-update-slice_fusion, bf16[16,8,3584]{2,1,0:T(8,128)(2,1)S(1)} %all-to-all-done.2), kind=kOutput, calls=%fused_computation.74 | convolution fusion | flops 1879048192 | bytes 16646144 | tf_op jit(solution)/shard_map/dot_general | solution.py:41
  317.5 5.2 %fusion.7 = bf16[16,8,3584]{2,1,0:T(8,128)(2,1)} fusion(bf16[1024,3584]{1,0:T(8,128)(2,1)} %constant_dynamic-update-slice_fusion.6, f32[128,2048]{1,0:T(8,128)S(1)} %fusion.47), kind=kOutput, calls=%fused_computation.19 | convolution fusion | flops 940769280 | bytes 9306112 | tf_op jit(solution)/shard_map/dot_general | solution.py:43
  322.7 12.3 %all-to-all-done.6 = bf16[16,8,3584]{2,1,0:T(8,128)(2,1)S(1)} async-done(((bf16[16,8,3584]{2,1,0:T(8,128)(2,1)}), bf16[16,8,3584]{2,1,0:T(8,128)(2,1)S(1)}, u32[]{:S(2)}, u32[]{:S(2)}) %all-to-all-start.6) | async-done | bytes 917536 | tf_op jit(solution)/shard_map/all_to_all | solution.py:62
  335.0 3.5 all-to-all-start.3
  338.6 7.2 %fusion.41 = f32[128,2048]{1,0:T(8,128)S(1)} fusion(bf16[3584,2048]{1,0:T(8,128)(2,1)} %maximum_dynamic-update-slice_fusion, bf16[16,8,3584]{2,1,0:T(8,128)(2,1)S(1)} %all-to-all-done.6), kind=kOutput, calls=%fused_computation.68 | convolution fusion | flops 1879048192 | bytes 16646144 | tf_op jit(solution)/shard_map/dot_general | solution.py:41
  345.8 5.2 %fusion.11 = bf16[16,8,3584]{2,1,0:T(8,128)(2,1)} fusion(bf16[1024,3584]{1,0:T(8,128)(2,1)} %constant_dynamic-update-slice_fusion.6, f32[128,2048]{1,0:T(8,128)S(1)} %fusion.41), kind=kOutput, calls=%fused_computation.23 | convolution fusion | flops 940769280 | bytes 9306112 | tf_op jit(solution)/shard_map/dot_general | solution.py:43
  351.0 12.7 %all-to-all-done.3 = bf16[16,8,3584]{2,1,0:T(8,128)(2,1)S(1)} async-done(((bf16[16,8,3584]{2,1,0:T(8,128)(2,1)}), bf16[16,8,3584]{2,1,0:T(8,128)(2,1)S(1)}, u32[]{:S(2)}, u32[]{:S(2)}) %all-to-all-start.3) | async-done | bytes 917536 | tf_op jit(solution)/shard_map/all_to_all | solution.py:64
  363.7 3.5 all-to-all-start.7
  369.6 22.7 %all-to-all-done.7 = bf16[16,8,3584]{2,1,0:T(8,128)(2,1)S(1)} async-done(((bf16[16,8,3584]{2,1,0:T(8,128)(2,1)}), bf16[16,8,3584]{2,1,0:T(8,128)(2,1)S(1)}, u32[]{:S(2)}, u32[]{:S(2)}) %all-to-all-start.7) | async-done | bytes 917536 | tf_op jit(solution)/shard_map/all_to_all | solution.py:64
  393.9 10.8 %collective-permute-done.15 = bf16[64,3584]{1,0:T(8,128)(2,1)S(1)} collective-permute-done((bf16[64,3584]{1,0:T(8,128)(2,1)S(1)}, bf16[64,3584]{1,0:T(8,128)(2,1)S(1)}, u32[]{:S(2)}, u32[]{:S(2)}) %collective-permute-start.15) | collective-permute-done | bytes 458784 | tf_op jit(solution)/shard_map/ppermute | solution.py:14
  (82 shorter events, 26.3 us)
Async XLA Ops:
  0.0 252.8 %copy-start = (bf16[1,3584,16]{1,2,0:T(8,128)(2,1)S(1)}, bf16[1,3584,16]{1,2,0:T(8,128)(2,1)}, u32[]{:S(2)}) copy-start(bf16[1,3584,16]{1,2,0:T(8,128)(2,1)} %param.9) | copy-start | bytes 344068
  0.0 41.7 %collective-permute-start = (bf16[3584,256]{1,0:T(8,128)(2,1)}, bf16[3584,256]{1,0:T(8,128)(2,1)}, u32[]{:S(2)}, u32[]{:S(2)}) collective-permute-start(bf16[3584,256]{1,0:T(8,128)(2,1)} %bitcast.119), channel_id=1, source_target_pairs={{0,16},{16,32},{32,48},{48,0},{1,17},{17,33},{33,49},{49,1},{2,18}... | collective-permute-start | bytes 5505032 | tf_op jit(solution)/shard_map/ppermute | solution.py:14
  2.1 45.6 %collective-permute-start.1 = (bf16[3584,256]{1,0:T(8,128)(2,1)}, bf16[3584,256]{1,0:T(8,128)(2,1)}, u32[]{:S(2)}, u32[]{:S(2)}) collective-permute-start(bf16[3584,256]{1,0:T(8,128)(2,1)} %bitcast.120), channel_id=1, source_target_pairs={{0,48},{16,0},{32,16},{48,32},{1,49},{17,1},{33,17},{49,33},{2,50}... | collective-permute-start | bytes 5505032 | tf_op jit(solution)/shard_map/ppermute | solution.py:14
  3.6 77.2 %collective-permute-start.4 = (bf16[3584,256]{1,0:T(8,128)(2,1)}, bf16[3584,256]{1,0:T(8,128)(2,1)S(1)}, u32[]{:S(2)}, u32[]{:S(2)}) collective-permute-start(bf16[3584,256]{1,0:T(8,128)(2,1)} %bitcast.123), channel_id=1, source_target_pairs={{0,16},{16,32},{32,48},{48,0},{1,17},{17,33},{33,49},{49,1},{2,18}... | collective-permute-start | bytes 5505032 | tf_op jit(solution)/shard_map/ppermute | solution.py:14
  3.6 80.5 %collective-permute-start.5 = (bf16[3584,256]{1,0:T(8,128)(2,1)}, bf16[3584,256]{1,0:T(8,128)(2,1)}, u32[]{:S(2)}, u32[]{:S(2)}) collective-permute-start(bf16[3584,256]{1,0:T(8,128)(2,1)} %bitcast.124), channel_id=1, source_target_pairs={{0,48},{16,0},{32,16},{48,32},{1,49},{17,1},{33,17},{49,33},{2,50}... | collective-permute-start | bytes 5505032 | tf_op jit(solution)/shard_map/ppermute | solution.py:14
  13.5 170.1 %all-to-all-start = ((bf16[16,8,3584]{2,1,0:T(8,128)(2,1)}), bf16[16,8,3584]{2,1,0:T(8,128)(2,1)S(1)}, u32[]{:S(2)}, u32[]{:S(2)}) async-start(bf16[16,8,3584]{2,1,0:T(8,128)(2,1)} %fusion.4), calls=%async_computation | async-start | bytes 1835008 | tf_op jit(solution)/shard_map/all_to_all | solution.py:62
  23.6 96.6 %collective-permute-start.8 = (bf16[256,3584]{1,0:T(8,128)(2,1)}, bf16[256,3584]{1,0:T(8,128)(2,1)S(1)}, u32[]{:S(2)}, u32[]{:S(2)}) collective-permute-start(bf16[256,3584]{1,0:T(8,128)(2,1)} %bitcast.121), channel_id=1, source_target_pairs={{0,16},{16,32},{32,48},{48,0},{1,17},{17,33},{33,49},{49,1},{2,18}... | collective-permute-start | bytes 5505032 | tf_op jit(solution)/shard_map/ppermute | solution.py:14
  41.7 87.6 %collective-permute-start.9 = (bf16[256,3584]{1,0:T(8,128)(2,1)}, bf16[256,3584]{1,0:T(8,128)(2,1)S(1)}, u32[]{:S(2)}, u32[]{:S(2)}) collective-permute-start(bf16[256,3584]{1,0:T(8,128)(2,1)} %bitcast.122), channel_id=1, source_target_pairs={{0,48},{16,0},{32,16},{48,32},{1,49},{17,1},{33,17},{49,33},{2,50}... | collective-permute-start | bytes 5505032 | tf_op jit(solution)/shard_map/ppermute | solution.py:14
  47.7 92.2 %collective-permute-start.2 = (bf16[1792,256]{1,0:T(8,128)(2,1)S(1)}, bf16[1792,256]{1,0:T(8,128)(2,1)S(1)}, u32[]{:S(2)}, u32[]{:S(2)}) collective-permute-start(bf16[1792,256]{1,0:T(8,128)(2,1)S(1)} %split.24), channel_id=1, source_target_pairs={{0,16},{16,32},{32,48},{48,0},{1,17},{17,33},{33,49},{49,1},{2,18}... | collective-permute-start | bytes 2752520 | tf_op jit(solution)/shard_map/ppermute | solution.py:14
  80.9 62.1 %collective-permute-start.3 = (bf16[1792,256]{1,0:T(8,128)(2,1)S(1)}, bf16[1792,256]{1,0:T(8,128)(2,1)S(1)}, u32[]{:S(2)}, u32[]{:S(2)}) collective-permute-start(bf16[1792,256]{1,0:T(8,128)(2,1)S(1)} %split.25), channel_id=1, source_target_pairs={{0,48},{16,0},{32,16},{48,32},{1,49},{17,1},{33,17},{49,33},{2,50}... | collective-permute-start | bytes 2752520 | tf_op jit(solution)/shard_map/ppermute | solution.py:14
  84.2 95.1 %collective-permute-start.6 = (bf16[1792,256]{1,0:T(8,128)(2,1)S(1)}, bf16[1792,256]{1,0:T(8,128)(2,1)S(1)}, u32[]{:S(2)}, u32[]{:S(2)}) collective-permute-start(bf16[1792,256]{1,0:T(8,128)(2,1)S(1)} %split.26), channel_id=1, source_target_pairs={{0,16},{16,32},{32,48},{48,0},{1,17},{17,33},{33,49},{49,1},{2,18}... | collective-permute-start | bytes 2752520 | tf_op jit(solution)/shard_map/ppermute | solution.py:14
  120.2 59.1 %collective-permute-start.7 = (bf16[1792,256]{1,0:T(8,128)(2,1)S(1)}, bf16[1792,256]{1,0:T(8,128)(2,1)S(1)}, u32[]{:S(2)}, u32[]{:S(2)}) collective-permute-start(bf16[1792,256]{1,0:T(8,128)(2,1)S(1)} %split.27), channel_id=1, source_target_pairs={{0,48},{16,0},{32,16},{48,32},{1,49},{17,1},{33,17},{49,33},{2,50}... | collective-permute-start | bytes 2752520 | tf_op jit(solution)/shard_map/ppermute | solution.py:14
  129.3 15.1 %copy-start.2 = (bf16[1,1,3584,256]{3,2,1,0:T(8,128)(2,1)S(1)}, bf16[1,1,3584,256]{3,2,1,0:T(8,128)(2,1)}, u32[]{:S(2)}) copy-start(bf16[1,1,3584,256]{3,2,1,0:T(8,128)(2,1)} %param.12) | copy-start | bytes 5505028
  129.3 49.9 %collective-permute-start.10 = (bf16[128,3584]{1,0:T(8,128)(2,1)S(1)}, bf16[128,3584]{1,0:T(8,128)(2,1)S(1)}, u32[]{:S(2)}, u32[]{:S(2)}) collective-permute-start(bf16[128,3584]{1,0:T(8,128)(2,1)S(1)} %split.28), channel_id=1, source_target_pairs={{0,16},{16,32},{32,48},{48,0},{1,17},{17,33},{33,49},{49,1},{2,18}... | collective-permute-start | bytes 2752520 | tf_op jit(solution)/shard_map/ppermute | solution.py:14
  139.9 55.4 %collective-permute-start.11 = (bf16[128,3584]{1,0:T(8,128)(2,1)}, bf16[128,3584]{1,0:T(8,128)(2,1)}, u32[]{:S(2)}, u32[]{:S(2)}) collective-permute-start(bf16[128,3584]{1,0:T(8,128)(2,1)} %split.29), channel_id=1, source_target_pairs={{0,48},{16,0},{32,16},{48,32},{1,49},{17,1},{33,17},{49,33},{2,50}... | collective-permute-start | bytes 2752520 | tf_op jit(solution)/shard_map/ppermute | solution.py:14
  179.2 2.9 copy-start.3
  183.6 37.0 %all-to-all-start.4 = ((bf16[16,8,3584]{2,1,0:T(8,128)(2,1)}), bf16[16,8,3584]{2,1,0:T(8,128)(2,1)S(1)}, u32[]{:S(2)}, u32[]{:S(2)}) async-start(bf16[16,8,3584]{2,1,0:T(8,128)(2,1)} %fusion.8), calls=%async_computation.4 | async-start | bytes 1835008 | tf_op jit(solution)/shard_map/all_to_all | solution.py:62
  197.4 7.4 %copy-start.4 = (bf16[1024,3584]{1,0:T(8,128)(2,1)S(1)}, bf16[1024,3584]{1,0:T(8,128)(2,1)}, u32[]{:S(2)}) copy-start(bf16[1024,3584]{1,0:T(8,128)(2,1)} %constant_dynamic-update-slice_fusion.6) | copy-start | bytes 22020100
  220.6 28.6 %all-to-all-start.1 = ((bf16[16,8,3584]{2,1,0:T(8,128)(2,1)}), bf16[16,8,3584]{2,1,0:T(8,128)(2,1)S(1)}, u32[]{:S(2)}, u32[]{:S(2)}) async-start(bf16[16,8,3584]{2,1,0:T(8,128)(2,1)} %fusion.5), calls=%async_computation.1 | async-start | bytes 1835008 | tf_op jit(solution)/shard_map/all_to_all | solution.py:64
  231.4 21.4 %copy-start.1 = (bf16[1,2,64,3584]{3,2,1,0:T(8,128)(2,1)S(1)}, bf16[1,2,64,3584]{3,2,1,0:T(8,128)(2,1)}, u32[]{:S(2)}) copy-start(bf16[1,2,64,3584]{3,2,1,0:T(8,128)(2,1)} %param.7) | copy-start | bytes 2752516
  249.2 28.6 %all-to-all-start.5 = ((bf16[16,8,3584]{2,1,0:T(8,128)(2,1)}), bf16[16,8,3584]{2,1,0:T(8,128)(2,1)S(1)}, u32[]{:S(2)}, u32[]{:S(2)}) async-start(bf16[16,8,3584]{2,1,0:T(8,128)(2,1)} %fusion.9), calls=%async_computation.5 | async-start | bytes 1835008 | tf_op jit(solution)/shard_map/all_to_all | solution.py:64
  253.5 13.5 %collective-permute-start.12 = (bf16[64,3584]{1,0:T(8,128)(2,1)S(1)}, bf16[64,3584]{1,0:T(8,128)(2,1)S(1)}, u32[]{:S(2)}, u32[]{:S(2)}) collective-permute-start(bf16[64,3584]{1,0:T(8,128)(2,1)S(1)} %fusion.12), channel_id=1, source_target_pairs={{0,64},{64,128},{128,192},{192,0},{1,65},{65,129},{129,193},{193,1... | collective-permute-start | bytes 1376264 | tf_op jit(solution)/shard_map/ppermute | solution.py:14
  277.8 28.7 %all-to-all-start.2 = ((bf16[16,8,3584]{2,1,0:T(8,128)(2,1)}), bf16[16,8,3584]{2,1,0:T(8,128)(2,1)S(1)}, u32[]{:S(2)}, u32[]{:S(2)}) async-start(bf16[16,8,3584]{2,1,0:T(8,128)(2,1)} %fusion.6), calls=%async_computation.2 | async-start | bytes 1835008 | tf_op jit(solution)/shard_map/all_to_all | solution.py:62
  282.0 13.5 %collective-permute-start.14 = (bf16[64,3584]{1,0:T(8,128)(2,1)S(1)}, bf16[64,3584]{1,0:T(8,128)(2,1)S(1)}, u32[]{:S(2)}, u32[]{:S(2)}) collective-permute-start(bf16[64,3584]{1,0:T(8,128)(2,1)S(1)} %fusion.14), channel_id=1, source_target_pairs={{0,64},{64,128},{128,192},{192,0},{1,65},{65,129},{129,193},{193,1... | collective-permute-start | bytes 1376264 | tf_op jit(solution)/shard_map/ppermute | solution.py:14
  306.5 28.6 %all-to-all-start.6 = ((bf16[16,8,3584]{2,1,0:T(8,128)(2,1)}), bf16[16,8,3584]{2,1,0:T(8,128)(2,1)S(1)}, u32[]{:S(2)}, u32[]{:S(2)}) async-start(bf16[16,8,3584]{2,1,0:T(8,128)(2,1)} %fusion.10), calls=%async_computation.6 | async-start | bytes 1835008 | tf_op jit(solution)/shard_map/all_to_all | solution.py:62
  335.0 28.7 %all-to-all-start.3 = ((bf16[16,8,3584]{2,1,0:T(8,128)(2,1)}), bf16[16,8,3584]{2,1,0:T(8,128)(2,1)S(1)}, u32[]{:S(2)}, u32[]{:S(2)}) async-start(bf16[16,8,3584]{2,1,0:T(8,128)(2,1)} %fusion.7), calls=%async_computation.3 | async-start | bytes 1835008 | tf_op jit(solution)/shard_map/all_to_all | solution.py:64
  363.7 28.6 %all-to-all-start.7 = ((bf16[16,8,3584]{2,1,0:T(8,128)(2,1)}), bf16[16,8,3584]{2,1,0:T(8,128)(2,1)S(1)}, u32[]{:S(2)}, u32[]{:S(2)}) async-start(bf16[16,8,3584]{2,1,0:T(8,128)(2,1)} %fusion.11), calls=%async_computation.7 | async-start | bytes 1835008 | tf_op jit(solution)/shard_map/all_to_all | solution.py:64
  368.3 25.6 %collective-permute-start.13 = (bf16[64,3584]{1,0:T(8,128)(2,1)S(1)}, bf16[64,3584]{1,0:T(8,128)(2,1)S(1)}, u32[]{:S(2)}, u32[]{:S(2)}) collective-permute-start(bf16[64,3584]{1,0:T(8,128)(2,1)S(1)} %fusion.13), channel_id=1, source_target_pairs={{0,64},{64,128},{128,192},{192,0},{1,65},{65,129},{129,193},{193,1... | collective-permute-start | bytes 1376264 | tf_op jit(solution)/shard_map/ppermute | solution.py:14
  392.6 12.1 %collective-permute-start.15 = (bf16[64,3584]{1,0:T(8,128)(2,1)S(1)}, bf16[64,3584]{1,0:T(8,128)(2,1)S(1)}, u32[]{:S(2)}, u32[]{:S(2)}) collective-permute-start(bf16[64,3584]{1,0:T(8,128)(2,1)S(1)} %fusion.15), channel_id=1, source_target_pairs={{0,64},{64,128},{128,192},{192,0},{1,65},{65,129},{129,193},{193,1... | collective-permute-start | bytes 1376264 | tf_op jit(solution)/shard_map/ppermute | solution.py:14
where the time goes:
time: 407 us; the launch traced here: 406 us
  waiting for transfers between devices  245 us (60%)
  starting transfers between devices  67.4 us (17%)
  matrix products  57.2 us (14%)
  local copies, waits for them, and re-layouts  27.7 us (7%)
  other arithmetic  7.68 us (2%)
    ppermute x16, waiting for transfers between devices, passed_along(): return lax.ppermute(value, axis, pairs)  153 us
    all_to_all x4, waiting for transfers between devices, apply_layer(): lax.all_to_all(summed.reshape(row_size, capacity, width), ROW, split_axis...  57.1 us
    all_to_all x4, waiting for transfers between devices, apply_layer(): lax.all_to_all(outbox, ROW, split_axis=0, concat_axis=0, tiled=True)  35.3 us
    dot_general x4, matrix products, expert_compute(): both = jnp.dot(rows_in, gate_up, preferred_element_type=jnp.float32)  29.1 us
    all_to_all x4, starting transfers between devices, apply_layer(): lax.all_to_all(outbox, ROW, split_axis=0, concat_axis=0, tiled=True)  29.1 us
    ppermute x16, starting transfers between devices, passed_along(): return lax.ppermute(value, axis, pairs)  24.2 us
    unnamed x20, local copies, waits for them, and re-layouts  19.4 us
    dot_general x4, matrix products, expert_compute(): jnp.dot(hidden, down_all, preferred_element_type=jnp.float32)  17.9 us
  transfers between devices with their start and end apart: 24, of which 15 were waited for; matrix products, arithmetic and copies ran while one was open for 22% of the time, Pallas kernels for 0%

commit v1 on v0

--- a/solution.py
+++ b/solution.py
@@ -42,7 +42,7 @@
         hidden = (jax.nn.silu(both[:, :hid_total]) * both[:, hid_total:]).astype(jnp.bfloat16)
         return jnp.dot(hidden, down_all, preferred_element_type=jnp.float32).astype(jnp.bfloat16)
 
-    def apply_layer(tokens_in, route_ids):
+    def prepare(tokens_in, route_ids):
         x_float = tokens_in.astype(jnp.float32)
         mean_sq = jnp.mean(x_float * x_float, axis=1, keepdims=True)
         normed = (x_float * lax.rsqrt(mean_sq + 1e-06) * gain_row[None, :]).astype(jnp.bfloat16)
@@ -58,8 +58,9 @@
             flat_slot[None, :] == jnp.arange(experts_here * capacity, dtype=jnp.int32)[:, None]
         ).astype(jnp.bfloat16)
         outbox = jnp.dot(placing, normed, preferred_element_type=jnp.float32).astype(jnp.bfloat16)
-        outbox = outbox.reshape(row_size, capacity, width)
-        arrived = lax.all_to_all(outbox, ROW, split_axis=0, concat_axis=0, tiled=True)
+        return x_float, gate_val, placing, outbox.reshape(row_size, capacity, width)
+
+    def finish(arrived, x_float, gate_val, placing):
         summed = expert_compute(arrived.reshape(-1, width))
         back = lax.all_to_all(
             summed.reshape(row_size, capacity, width), ROW, split_axis=0, concat_axis=0, tiled=True
@@ -72,9 +73,19 @@
     micro_count = acts.shape[1]
     carried = [acts[0, micro_idx] for micro_idx in range(micro_count)]
     for round_idx in range(routes.shape[1]):
+        ready = [prepare(carried[m], routes[0, round_idx, m]) for m in range(micro_count)]
+        if round_idx == 0:
+            stacked = jnp.stack([parts[3] for parts in ready], axis=1)
+            together = lax.all_to_all(stacked, ROW, split_axis=0, concat_axis=0, tiled=True)
+            arrivals = [together[:, m] for m in range(micro_count)]
+        else:
+            arrivals = [
+                lax.all_to_all(parts[3], ROW, split_axis=0, concat_axis=0, tiled=True)
+                for parts in ready
+            ]
         carried = [
-            passed_along(apply_layer(carried[micro_idx], routes[0, round_idx, micro_idx]), "section", 1)
-            for micro_idx in range(micro_count)
+            passed_along(finish(arrivals[m], *ready[m][:3]), "section", 1)
+            for m in range(micro_count)
         ]
     return jnp.stack(carried)[None]
 

time: 407 us -> 392 us (0.963)
  waiting for transfers between devices: 245 us -> 235 us
    all_to_all x8 -> x7, waiting for transfers between devices: 92.4 us -> 78 us  [the longest x4 56.3 us: finish(): lax.all_to_all(summed.reshape(row_size, capacity, width), ROW, split_axis...]
    ppermute x16, waiting for transfers between devices: 153 us -> 157 us  [passed_along(): return lax.ppermute(value, axis, pairs)]
    all_to_all x8 -> x7, starting transfers between devices: 43.2 us -> 39.7 us  [the longest x4 22.3 us: finish(): lax.all_to_all(summed.reshape(row_size, capacity, width), ROW, split_axis...]
  transfers between devices with their start and end apart: 24 -> 23, of which waited for: 15 -> 14; matrix products, arithmetic and copies ran while one was open for 22% -> 21% of each run, Pallas kernels for 0% -> 0%
where the time goes in v1:
time: 392 us; the launch traced here: 391 us
  waiting for transfers between devices  235 us (60%)
  starting transfers between devices  63.7 us (16%)
  matrix products  56.5 us (14%)
  local copies, waits for them, and re-layouts  25.9 us (7%)
  other arithmetic  9.11 us (2%)
    ppermute x16, waiting for transfers between devices, passed_along(): return lax.ppermute(value, axis, pairs)  157 us
    all_to_all x4, waiting for transfers between devices, finish(): lax.all_to_all(summed.reshape(row_size, capacity, width), ROW, split_axis...  56.3 us
    dot_general x4, matrix products, expert_compute(): both = jnp.dot(rows_in, gate_up, preferred_element_type=jnp.float32)  29.1 us
    ppermute x16, starting transfers between devices, passed_along(): return lax.ppermute(value, axis, pairs)  24.1 us
    all_to_all x4, starting transfers between devices, finish(): lax.all_to_all(summed.reshape(row_size, capacity, width), ROW, split_axis...  22.3 us
    all_to_all x2, waiting for transfers between devices, body(): lax.all_to_all(parts[3], ROW, split_axis=0, concat_axis=0, tiled=True)  21.7 us
    unnamed x20, local copies, waits for them, and re-layouts  19.4 us
    dot_general x4, matrix products, expert_compute(): jnp.dot(hidden, down_all, preferred_element_type=jnp.float32)  17.9 us
  transfers between devices with their start and end apart: 23, of which 14 were waited for; matrix products, arithmetic and copies ran while one was open for 21% of the time, Pallas kernels for 0%

profile of v1, /device:TPU:1, one launch (start us, length us, event | category | flops | bytes accessed | tf_op | source)
XLA Modules:
  0.0 391.0 jit_solution(4023029861409219269)
XLA Ops:
  0.0 2.1 collective-permute-start
  2.1 1.5 collective-permute-start.1
  3.6 2.7 collective-permute-start.5
  8.1 1.4 fusion.24
  11.0 1.5 fusion.4
  12.5 1.5 fusion.5
  14.0 1.4 pad_maximum_fusion
  15.5 10.1 %all-to-all-start = ((bf16[16,2,8,3584]{3,2,1,0:T(8,128)(2,1)}), bf16[16,2,8,3584]{3,2,1,0:T(8,128)(2,1)S(1)}, u32[]{:S(2)}, u32[]{:S(2)}) async-start(bf16[16,2,8,3584]{3,2,1,0:T(8,128)(2,1)} %pad_maximum_fusion), calls=%async_computation | async-start | bytes 3670016 | tf_op jit(solution)/shard_map/all_to_all | solution.py:79
  25.6 2.9 constant_dynamic-update-slice_fusion.5
  28.5 13.1 %collective-permute-done = bf16[3584,256]{1,0:T(8,128)(2,1)} collective-permute-done((bf16[3584,256]{1,0:T(8,128)(2,1)}, bf16[3584,256]{1,0:T(8,128)(2,1)}, u32[]{:S(2)}, u32[]{:S(2)}) %collective-permute-start) | collective-permute-done | bytes 1835040 | tf_op jit(solution)/shard_map/ppermute | solution.py:14
  41.7 3.1 collective-permute-start.9
  44.8 1.7 constant_dynamic-update-slice_fusion.10
  49.0 32.0 %collective-permute-done.4 = bf16[3584,256]{1,0:T(8,128)(2,1)} collective-permute-done((bf16[3584,256]{1,0:T(8,128)(2,1)}, bf16[3584,256]{1,0:T(8,128)(2,1)}, u32[]{:S(2)}, u32[]{:S(2)}) %collective-permute-start.4) | collective-permute-done | bytes 1835040 | tf_op jit(solution)/shard_map/ppermute | solution.py:14
  81.0 3.1 collective-permute-start.3
  86.7 33.5 %collective-permute-done.8 = bf16[256,3584]{1,0:T(8,128)(2,1)S(1)} collective-permute-done((bf16[256,3584]{1,0:T(8,128)(2,1)}, bf16[256,3584]{1,0:T(8,128)(2,1)S(1)}, u32[]{:S(2)}, u32[]{:S(2)}) %collective-permute-start.8) | collective-permute-done | bytes 1835040 | tf_op jit(solution)/shard_map/ppermute | solution.py:14
  120.2 3.1 collective-permute-start.7
  123.4 3.0 constant_dynamic-update-slice_fusion.4
  126.3 2.9 constant_dynamic-update-slice_fusion.3
  129.6 10.3 %collective-permute-done.2 = bf16[1792,256]{1,0:T(8,128)(2,1)S(1)} collective-permute-done((bf16[1792,256]{1,0:T(8,128)(2,1)S(1)}, bf16[1792,256]{1,0:T(8,128)(2,1)S(1)}, u32[]{:S(2)}, u32[]{:S(2)}) %collective-permute-start.2) | collective-permute-done | bytes 917536 | tf_op jit(solution)/shard_map/ppermute | solution.py:14
  139.9 3.1 collective-permute-start.11
  143.0 1.4 maximum_dynamic-update-slice_fusion.1
  145.8 33.4 %collective-permute-done.10 = bf16[128,3584]{1,0:T(8,128)(2,1)S(1)} collective-permute-done((bf16[128,3584]{1,0:T(8,128)(2,1)S(1)}, bf16[128,3584]{1,0:T(8,128)(2,1)S(1)}, u32[]{:S(2)}, u32[]{:S(2)}) %collective-permute-start.10) | collective-permute-done | bytes 917536 | tf_op jit(solution)/shard_map/ppermute | solution.py:14
  179.2 2.9 constant_dynamic-update-slice_fusion.1
  182.2 4.3 %constant_dynamic-update-slice_fusion = bf16[3584,2048]{1,0:T(8,128)(2,1)} fusion(bf16[3584,2048]{1,0:T(8,128)(2,1)} %constant_dynamic-update-slice_fusion.1, bf16[3584,256]{1,0:T(8,128)(2,1)} %collective-permute-done.5), kind=kLoop, calls=%fused_computation.122 | loop fusion | bytes 3670016
  188.0 7.4 %fusion.41 = f32[128,2048]{1,0:T(8,128)S(1)} fusion(bf16[3584,2048]{1,0:T(8,128)(2,1)} %maximum_dynamic-update-slice_fusion, bf16[16,2,8,3584]{3,2,1,0:T(8,128)(2,1)S(1)} %all-to-all-done), kind=kOutput, calls=%fused_computation.70 | convolution fusion | flops 1879048192 | bytes 16646144 | tf_op jit(solution)/shard_map/dot_general | solution.py:41
  195.4 2.1 fusion.6
  197.5 11.7 %all-to-all-start.1 = ((bf16[16,8,3584]{2,1,0:T(8,128)(2,1)}), bf16[16,8,3584]{2,1,0:T(8,128)(2,1)}, u32[]{:S(2)}, u32[]{:S(2)}) async-start(bf16[16,8,3584]{2,1,0:T(8,128)(2,1)} %fusion.6), calls=%async_computation.1 | async-start | bytes 1835008 | tf_op jit(solution)/shard_map/all_to_all | solution.py:65
  209.1 7.2 %fusion.40 = f32[128,2048]{1,0:T(8,128)S(1)} fusion(bf16[3584,2048]{1,0:T(8,128)(2,1)} %maximum_dynamic-update-slice_fusion, bf16[16,2,8,3584]{3,2,1,0:T(8,128)(2,1)S(1)} %all-to-all-done), kind=kOutput, calls=%fused_computation.68 | convolution fusion | flops 1879048192 | bytes 16646144 | tf_op jit(solution)/shard_map/dot_general | solution.py:41
  216.4 5.3 %fusion.9 = bf16[16,8,3584]{2,1,0:T(8,128)(2,1)} fusion(bf16[1024,3584]{1,0:T(8,128)(2,1)} %copy-done.3, f32[128,2048]{1,0:T(8,128)S(1)} %fusion.40), kind=kOutput, calls=%fused_computation.21 | convolution fusion | flops 940769280 | bytes 9306112 | tf_op jit(solution)/shard_map/dot_general | solution.py:43
  221.7 12.9 %all-to-all-done.1 = bf16[16,8,3584]{2,1,0:T(8,128)(2,1)} async-done(((bf16[16,8,3584]{2,1,0:T(8,128)(2,1)}), bf16[16,8,3584]{2,1,0:T(8,128)(2,1)}, u32[]{:S(2)}, u32[]{:S(2)}) %all-to-all-start.1) | async-done | bytes 917536 | tf_op jit(solution)/shard_map/all_to_all | solution.py:65
  234.6 3.5 all-to-all-start.4
  238.5 1.5 fusion.12
  241.3 12.3 %collective-permute-done.12 = bf16[64,3584]{1,0:T(8,128)(2,1)S(1)} collective-permute-done((bf16[64,3584]{1,0:T(8,128)(2,1)S(1)}, bf16[64,3584]{1,0:T(8,128)(2,1)S(1)}, u32[]{:S(2)}, u32[]{:S(2)}) %collective-permute-start.12) | collective-permute-done | bytes 458784 | tf_op jit(solution)/shard_map/ppermute | solution.py:14
  255.2 8.0 %all-to-all-done.4 = bf16[16,8,3584]{2,1,0:T(8,128)(2,1)S(1)} async-done(((bf16[16,8,3584]{2,1,0:T(8,128)(2,1)}), bf16[16,8,3584]{2,1,0:T(8,128)(2,1)S(1)}, u32[]{:S(2)}, u32[]{:S(2)}) %all-to-all-start.4) | async-done | bytes 917536 | tf_op jit(solution)/shard_map/all_to_all | solution.py:65
  263.2 3.5 all-to-all-start.2
  268.7 12.2 %collective-permute-done.14 = bf16[64,3584]{1,0:T(8,128)(2,1)S(1)} collective-permute-done((bf16[64,3584]{1,0:T(8,128)(2,1)S(1)}, bf16[64,3584]{1,0:T(8,128)(2,1)S(1)}, u32[]{:S(2)}, u32[]{:S(2)}) %collective-permute-start.14) | collective-permute-done | bytes 458784 | tf_op jit(solution)/shard_map/ppermute | solution.py:14
  282.5 9.3 %all-to-all-done.2 = bf16[16,8,3584]{2,1,0:T(8,128)(2,1)S(1)} async-done(((bf16[16,8,3584]{2,1,0:T(8,128)(2,1)}), bf16[16,8,3584]{2,1,0:T(8,128)(2,1)S(1)}, u32[]{:S(2)}, u32[]{:S(2)}) %all-to-all-start.2) | async-done | bytes 917536 | tf_op jit(solution)/shard_map/all_to_all | solution.py:83
  291.8 3.8 all-to-all-start.5
  295.6 7.2 %fusion.47 = f32[128,2048]{1,0:T(8,128)S(1)} fusion(bf16[3584,2048]{1,0:T(8,128)(2,1)} %maximum_dynamic-update-slice_fusion, bf16[16,8,3584]{2,1,0:T(8,128)(2,1)S(1)} %all-to-all-done.2), kind=kOutput, calls=%fused_computation.77 | convolution fusion | flops 1879048192 | bytes 16646144 | tf_op jit(solution)/shard_map/dot_general | solution.py:41
  302.8 5.2 %fusion.8 = bf16[16,8,3584]{2,1,0:T(8,128)(2,1)} fusion(bf16[1024,3584]{1,0:T(8,128)(2,1)} %copy-done.3, f32[128,2048]{1,0:T(8,128)S(1)} %fusion.47), kind=kOutput, calls=%fused_computation.20 | convolution fusion | flops 940769280 | bytes 9306112 | tf_op jit(solution)/shard_map/dot_general | solution.py:43
  308.1 12.3 %all-to-all-done.5 = bf16[16,8,3584]{2,1,0:T(8,128)(2,1)S(1)} async-done(((bf16[16,8,3584]{2,1,0:T(8,128)(2,1)}), bf16[16,8,3584]{2,1,0:T(8,128)(2,1)S(1)}, u32[]{:S(2)}, u32[]{:S(2)}) %all-to-all-start.5) | async-done | bytes 917536 | tf_op jit(solution)/shard_map/all_to_all | solution.py:83
  320.4 3.5 all-to-all-start.3
  323.9 7.2 %fusion.43 = f32[128,2048]{1,0:T(8,128)S(1)} fusion(bf16[3584,2048]{1,0:T(8,128)(2,1)} %maximum_dynamic-update-slice_fusion, bf16[16,8,3584]{2,1,0:T(8,128)(2,1)S(1)} %all-to-all-done.5), kind=kOutput, calls=%fused_computation.73 | convolution fusion | flops 1879048192 | bytes 16646144 | tf_op jit(solution)/shard_map/dot_general | solution.py:41
  331.2 5.2 %fusion.11 = bf16[16,8,3584]{2,1,0:T(8,128)(2,1)} fusion(bf16[1024,3584]{1,0:T(8,128)(2,1)} %copy-done.3, f32[128,2048]{1,0:T(8,128)S(1)} %fusion.43), kind=kOutput, calls=%fused_computation.23 | convolution fusion | flops 940769280 | bytes 9306112 | tf_op jit(solution)/shard_map/dot_general | solution.py:43
  336.4 12.7 %all-to-all-done.3 = bf16[16,8,3584]{2,1,0:T(8,128)(2,1)S(1)} async-done(((bf16[16,8,3584]{2,1,0:T(8,128)(2,1)}), bf16[16,8,3584]{2,1,0:T(8,128)(2,1)S(1)}, u32[]{:S(2)}, u32[]{:S(2)}) %all-to-all-start.3) | async-done | bytes 917536 | tf_op jit(solution)/shard_map/all_to_all | solution.py:65
  349.1 3.5 all-to-all-start.6
  354.9 22.7 %all-to-all-done.6 = bf16[16,8,3584]{2,1,0:T(8,128)(2,1)S(1)} async-done(((bf16[16,8,3584]{2,1,0:T(8,128)(2,1)}), bf16[16,8,3584]{2,1,0:T(8,128)(2,1)S(1)}, u32[]{:S(2)}, u32[]{:S(2)}) %all-to-all-start.6) | async-done | bytes 917536 | tf_op jit(solution)/shard_map/all_to_all | solution.py:65
  379.3 10.8 %collective-permute-done.15 = bf16[64,3584]{1,0:T(8,128)(2,1)S(1)} collective-permute-done((bf16[64,3584]{1,0:T(8,128)(2,1)S(1)}, bf16[64,3584]{1,0:T(8,128)(2,1)S(1)}, u32[]{:S(2)}, u32[]{:S(2)}) %collective-permute-start.15) | collective-permute-done | bytes 458784 | tf_op jit(solution)/shard_map/ppermute | solution.py:14
  (80 shorter events, 23.4 us)
Async XLA Ops:
  0.0 238.2 %copy-start = (bf16[1,3584,16]{1,2,0:T(8,128)(2,1)S(1)}, bf16[1,3584,16]{1,2,0:T(8,128)(2,1)}, u32[]{:S(2)}) copy-start(bf16[1,3584,16]{1,2,0:T(8,128)(2,1)} %param.9) | copy-start | bytes 344068
  0.0 41.7 %collective-permute-start = (bf16[3584,256]{1,0:T(8,128)(2,1)}, bf16[3584,256]{1,0:T(8,128)(2,1)}, u32[]{:S(2)}, u32[]{:S(2)}) collective-permute-start(bf16[3584,256]{1,0:T(8,128)(2,1)} %bitcast.123), channel_id=1, source_target_pairs={{0,16},{16,32},{32,48},{48,0},{1,17},{17,33},{33,49},{49,1},{2,18}... | collective-permute-start | bytes 5505032 | tf_op jit(solution)/shard_map/ppermute | solution.py:14
  2.1 45.6 %collective-permute-start.1 = (bf16[3584,256]{1,0:T(8,128)(2,1)}, bf16[3584,256]{1,0:T(8,128)(2,1)}, u32[]{:S(2)}, u32[]{:S(2)}) collective-permute-start(bf16[3584,256]{1,0:T(8,128)(2,1)} %bitcast.124), channel_id=1, source_target_pairs={{0,48},{16,0},{32,16},{48,32},{1,49},{17,1},{33,17},{49,33},{2,50}... | collective-permute-start | bytes 5505032 | tf_op jit(solution)/shard_map/ppermute | solution.py:14
  3.6 77.3 %collective-permute-start.4 = (bf16[3584,256]{1,0:T(8,128)(2,1)}, bf16[3584,256]{1,0:T(8,128)(2,1)}, u32[]{:S(2)}, u32[]{:S(2)}) collective-permute-start(bf16[3584,256]{1,0:T(8,128)(2,1)} %bitcast.127), channel_id=1, source_target_pairs={{0,16},{16,32},{32,48},{48,0},{1,17},{17,33},{33,49},{49,1},{2,18}... | collective-permute-start | bytes 5505032 | tf_op jit(solution)/shard_map/ppermute | solution.py:14
  3.6 81.7 %collective-permute-start.5 = (bf16[3584,256]{1,0:T(8,128)(2,1)}, bf16[3584,256]{1,0:T(8,128)(2,1)}, u32[]{:S(2)}, u32[]{:S(2)}) collective-permute-start(bf16[3584,256]{1,0:T(8,128)(2,1)} %bitcast.128), channel_id=1, source_target_pairs={{0,48},{16,0},{32,16},{48,32},{1,49},{17,1},{33,17},{49,33},{2,50}... | collective-permute-start | bytes 5505032 | tf_op jit(solution)/shard_map/ppermute | solution.py:14
  15.5 172.5 %all-to-all-start = ((bf16[16,2,8,3584]{3,2,1,0:T(8,128)(2,1)}), bf16[16,2,8,3584]{3,2,1,0:T(8,128)(2,1)S(1)}, u32[]{:S(2)}, u32[]{:S(2)}) async-start(bf16[16,2,8,3584]{3,2,1,0:T(8,128)(2,1)} %pad_maximum_fusion), calls=%async_computation | async-start | bytes 3670016 | tf_op jit(solution)/shard_map/all_to_all | solution.py:79
  25.6 94.6 %collective-permute-start.8 = (bf16[256,3584]{1,0:T(8,128)(2,1)}, bf16[256,3584]{1,0:T(8,128)(2,1)S(1)}, u32[]{:S(2)}, u32[]{:S(2)}) collective-permute-start(bf16[256,3584]{1,0:T(8,128)(2,1)} %bitcast.125), channel_id=1, source_target_pairs={{0,16},{16,32},{32,48},{48,0},{1,17},{17,33},{33,49},{49,1},{2,18}... | collective-permute-start | bytes 5505032 | tf_op jit(solution)/shard_map/ppermute | solution.py:14
  41.7 87.6 %collective-permute-start.9 = (bf16[256,3584]{1,0:T(8,128)(2,1)}, bf16[256,3584]{1,0:T(8,128)(2,1)S(1)}, u32[]{:S(2)}, u32[]{:S(2)}) collective-permute-start(bf16[256,3584]{1,0:T(8,128)(2,1)} %bitcast.126), channel_id=1, source_target_pairs={{0,48},{16,0},{32,16},{48,32},{1,49},{17,1},{33,17},{49,33},{2,50}... | collective-permute-start | bytes 5505032 | tf_op jit(solution)/shard_map/ppermute | solution.py:14
  47.7 92.2 %collective-permute-start.2 = (bf16[1792,256]{1,0:T(8,128)(2,1)S(1)}, bf16[1792,256]{1,0:T(8,128)(2,1)S(1)}, u32[]{:S(2)}, u32[]{:S(2)}) collective-permute-start(bf16[1792,256]{1,0:T(8,128)(2,1)S(1)} %split.24), channel_id=1, source_target_pairs={{0,16},{16,32},{32,48},{48,0},{1,17},{17,33},{33,49},{49,1},{2,18}... | collective-permute-start | bytes 2752520 | tf_op jit(solution)/shard_map/ppermute | solution.py:14
  81.0 62.0 %collective-permute-start.3 = (bf16[1792,256]{1,0:T(8,128)(2,1)S(1)}, bf16[1792,256]{1,0:T(8,128)(2,1)S(1)}, u32[]{:S(2)}, u32[]{:S(2)}) collective-permute-start(bf16[1792,256]{1,0:T(8,128)(2,1)S(1)} %split.25), channel_id=1, source_target_pairs={{0,48},{16,0},{32,16},{48,32},{1,49},{17,1},{33,17},{49,33},{2,50}... | collective-permute-start | bytes 2752520 | tf_op jit(solution)/shard_map/ppermute | solution.py:14
  85.3 101.2 %collective-permute-start.6 = (bf16[1792,256]{1,0:T(8,128)(2,1)S(1)}, bf16[1792,256]{1,0:T(8,128)(2,1)S(1)}, u32[]{:S(2)}, u32[]{:S(2)}) collective-permute-start(bf16[1792,256]{1,0:T(8,128)(2,1)S(1)} %split.26), channel_id=1, source_target_pairs={{0,16},{16,32},{32,48},{48,0},{1,17},{17,33},{33,49},{49,1},{2,18}... | collective-permute-start | bytes 2752520 | tf_op jit(solution)/shard_map/ppermute | solution.py:14
  120.2 66.3 %collective-permute-start.7 = (bf16[1792,256]{1,0:T(8,128)(2,1)S(1)}, bf16[1792,256]{1,0:T(8,128)(2,1)S(1)}, u32[]{:S(2)}, u32[]{:S(2)}) collective-permute-start(bf16[1792,256]{1,0:T(8,128)(2,1)S(1)} %split.27), channel_id=1, source_target_pairs={{0,48},{16,0},{32,16},{48,32},{1,49},{17,1},{33,17},{49,33},{2,50}... | collective-permute-start | bytes 2752520 | tf_op jit(solution)/shard_map/ppermute | solution.py:14
  129.3 15.1 %copy-start.2 = (bf16[1,1,3584,256]{3,2,1,0:T(8,128)(2,1)S(1)}, bf16[1,1,3584,256]{3,2,1,0:T(8,128)(2,1)}, u32[]{:S(2)}) copy-start(bf16[1,1,3584,256]{3,2,1,0:T(8,128)(2,1)} %param.12) | copy-start | bytes 5505028
  129.3 49.9 %collective-permute-start.10 = (bf16[128,3584]{1,0:T(8,128)(2,1)S(1)}, bf16[128,3584]{1,0:T(8,128)(2,1)S(1)}, u32[]{:S(2)}, u32[]{:S(2)}) collective-permute-start(bf16[128,3584]{1,0:T(8,128)(2,1)S(1)} %split.28), channel_id=1, source_target_pairs={{0,16},{16,32},{32,48},{48,0},{1,17},{17,33},{33,49},{49,1},{2,18}... | collective-permute-start | bytes 2752520 | tf_op jit(solution)/shard_map/ppermute | solution.py:14
  139.9 42.3 %collective-permute-start.11 = (bf16[128,3584]{1,0:T(8,128)(2,1)S(1)}, bf16[128,3584]{1,0:T(8,128)(2,1)S(1)}, u32[]{:S(2)}, u32[]{:S(2)}) collective-permute-start(bf16[128,3584]{1,0:T(8,128)(2,1)S(1)} %split.29), channel_id=1, source_target_pairs={{0,48},{16,0},{32,16},{48,32},{1,49},{17,1},{33,17},{49,33},{2,50}... | collective-permute-start | bytes 2752520 | tf_op jit(solution)/shard_map/ppermute | solution.py:14
  182.2 4.3 %copy-start.3 = (bf16[1024,3584]{1,0:T(8,128)(2,1)}, bf16[1024,3584]{1,0:T(8,128)(2,1)S(1)}, u32[]{:S(2)}) copy-start(bf16[1024,3584]{1,0:T(8,128)(2,1)S(1)} %constant_dynamic-update-slice_fusion.6) | copy-start | bytes 22020100
  188.0 7.4 %copy-start.4 = (bf16[1024,3584]{1,0:T(8,128)(2,1)S(1)}, bf16[1024,3584]{1,0:T(8,128)(2,1)}, u32[]{:S(2)}) copy-start(bf16[1024,3584]{1,0:T(8,128)(2,1)} %copy-done.3) | copy-start | bytes 22020100
  197.5 37.1 %all-to-all-start.1 = ((bf16[16,8,3584]{2,1,0:T(8,128)(2,1)}), bf16[16,8,3584]{2,1,0:T(8,128)(2,1)}, u32[]{:S(2)}, u32[]{:S(2)}) async-start(bf16[16,8,3584]{2,1,0:T(8,128)(2,1)} %fusion.6), calls=%async_computation.1 | async-start | bytes 1835008 | tf_op jit(solution)/shard_map/all_to_all | solution.py:65
  216.4 21.8 %copy-start.1 = (bf16[1,2,64,3584]{3,2,1,0:T(8,128)(2,1)S(1)}, bf16[1,2,64,3584]{3,2,1,0:T(8,128)(2,1)}, u32[]{:S(2)}) copy-start(bf16[1,2,64,3584]{3,2,1,0:T(8,128)(2,1)} %param.7) | copy-start | bytes 2752516
  234.6 28.6 %all-to-all-start.4 = ((bf16[16,8,3584]{2,1,0:T(8,128)(2,1)}), bf16[16,8,3584]{2,1,0:T(8,128)(2,1)S(1)}, u32[]{:S(2)}, u32[]{:S(2)}) async-start(bf16[16,8,3584]{2,1,0:T(8,128)(2,1)} %fusion.9), calls=%async_computation.4 | async-start | bytes 1835008 | tf_op jit(solution)/shard_map/all_to_all | solution.py:65
  240.0 13.5 %collective-permute-start.12 = (bf16[64,3584]{1,0:T(8,128)(2,1)S(1)}, bf16[64,3584]{1,0:T(8,128)(2,1)S(1)}, u32[]{:S(2)}, u32[]{:S(2)}) collective-permute-start(bf16[64,3584]{1,0:T(8,128)(2,1)S(1)} %fusion.12), channel_id=1, source_target_pairs={{0,64},{64,128},{128,192},{192,0},{1,65},{65,129},{129,193},{193,1... | collective-permute-start | bytes 1376264 | tf_op jit(solution)/shard_map/ppermute | solution.py:14
  263.2 28.7 %all-to-all-start.2 = ((bf16[16,8,3584]{2,1,0:T(8,128)(2,1)}), bf16[16,8,3584]{2,1,0:T(8,128)(2,1)S(1)}, u32[]{:S(2)}, u32[]{:S(2)}) async-start(bf16[16,8,3584]{2,1,0:T(8,128)(2,1)} %fusion.7), calls=%async_computation.2 | async-start | bytes 1835008 | tf_op jit(solution)/shard_map/all_to_all | solution.py:83
  267.4 13.5 %collective-permute-start.14 = (bf16[64,3584]{1,0:T(8,128)(2,1)S(1)}, bf16[64,3584]{1,0:T(8,128)(2,1)S(1)}, u32[]{:S(2)}, u32[]{:S(2)}) collective-permute-start(bf16[64,3584]{1,0:T(8,128)(2,1)S(1)} %fusion.14), channel_id=1, source_target_pairs={{0,64},{64,128},{128,192},{192,0},{1,65},{65,129},{129,193},{193,1... | collective-permute-start | bytes 1376264 | tf_op jit(solution)/shard_map/ppermute | solution.py:14
  291.8 28.6 %all-to-all-start.5 = ((bf16[16,8,3584]{2,1,0:T(8,128)(2,1)}), bf16[16,8,3584]{2,1,0:T(8,128)(2,1)S(1)}, u32[]{:S(2)}, u32[]{:S(2)}) async-start(bf16[16,8,3584]{2,1,0:T(8,128)(2,1)} %fusion.10), calls=%async_computation.5 | async-start | bytes 1835008 | tf_op jit(solution)/shard_map/all_to_all | solution.py:83
  320.4 28.7 %all-to-all-start.3 = ((bf16[16,8,3584]{2,1,0:T(8,128)(2,1)}), bf16[16,8,3584]{2,1,0:T(8,128)(2,1)S(1)}, u32[]{:S(2)}, u32[]{:S(2)}) async-start(bf16[16,8,3584]{2,1,0:T(8,128)(2,1)} %fusion.8), calls=%async_computation.3 | async-start | bytes 1835008 | tf_op jit(solution)/shard_map/all_to_all | solution.py:65
  349.1 28.6 %all-to-all-start.6 = ((bf16[16,8,3584]{2,1,0:T(8,128)(2,1)}), bf16[16,8,3584]{2,1,0:T(8,128)(2,1)S(1)}, u32[]{:S(2)}, u32[]{:S(2)}) async-start(bf16[16,8,3584]{2,1,0:T(8,128)(2,1)} %fusion.11), calls=%async_computation.6 | async-start | bytes 1835008 | tf_op jit(solution)/shard_map/all_to_all | solution.py:65
  353.6 25.6 %collective-permute-start.13 = (bf16[64,3584]{1,0:T(8,128)(2,1)S(1)}, bf16[64,3584]{1,0:T(8,128)(2,1)S(1)}, u32[]{:S(2)}, u32[]{:S(2)}) collective-permute-start(bf16[64,3584]{1,0:T(8,128)(2,1)S(1)} %fusion.13), channel_id=1, source_target_pairs={{0,64},{64,128},{128,192},{192,0},{1,65},{65,129},{129,193},{193,1... | collective-permute-start | bytes 1376264 | tf_op jit(solution)/shard_map/ppermute | solution.py:14
  378.0 12.1 %collective-permute-start.15 = (bf16[64,3584]{1,0:T(8,128)(2,1)S(1)}, bf16[64,3584]{1,0:T(8,128)(2,1)S(1)}, u32[]{:S(2)}, u32[]{:S(2)}) collective-permute-start(bf16[64,3584]{1,0:T(8,128)(2,1)S(1)} %fusion.15), channel_id=1, source_target_pairs={{0,64},{64,128},{128,192},{192,0},{1,65},{65,129},{129,193},{193,1... | collective-permute-start | bytes 1376264 | tf_op jit(solution)/shard_map/ppermute | solution.py:14

commit v2 on v1

--- a/solution.py
+++ b/solution.py
@@ -19,7 +19,7 @@
     from_above = passed_along(block, "y", -1)
     far_low = passed_along(jnp.split(from_below, 2, axis=axis)[0], "y", 1)
     far_high = passed_along(jnp.split(from_above, 2, axis=axis)[1], "y", -1)
-    return [block, from_below, from_above, jnp.concatenate([far_low, far_high], axis=axis)]
+    return [block, from_below, from_above], [far_low, far_high]
 
 
 def body(acts, norm_gain, router, routes, w_gate, w_up, w_down):
@@ -30,17 +30,25 @@
     capacity = 2 * tok_local // experts_here
     gain_row = norm_gain[0]
     router_mat = router[0]
-    gate_mats = gathered_blocks(w_gate[0, 0], 0)
-    up_mats = gathered_blocks(w_up[0, 0], 0)
-    down_mats = gathered_blocks(w_down[0, 0], 0)
-    hid_total = sum(mat.shape[1] for mat in gate_mats)
-    gate_up = jnp.concatenate(gate_mats + up_mats, axis=1)
-    down_all = jnp.concatenate(down_mats, axis=0)
+    gate_near, gate_far = gathered_blocks(w_gate[0, 0], 1)
+    up_near, up_far = gathered_blocks(w_up[0, 0], 1)
+    down_near, down_far = gathered_blocks(w_down[0, 0], 0)
+    near_hid = sum(mat.shape[1] for mat in gate_near)
+    far_hid = sum(mat.shape[1] for mat in gate_far)
+    near_gate_up = jnp.concatenate(gate_near + up_near, axis=1)
+    near_down = jnp.concatenate(down_near, axis=0)
+    far_gate_up = jnp.concatenate(gate_far + up_far, axis=1)
+    far_down = jnp.concatenate(down_far, axis=0)
+
+    def expert_part(rows_in, gate_up, down_all, hid):
+        both = jnp.dot(rows_in, gate_up, preferred_element_type=jnp.float32)
+        hidden = (jax.nn.silu(both[:, :hid]) * both[:, hid:]).astype(jnp.bfloat16)
+        return jnp.dot(hidden, down_all, preferred_element_type=jnp.float32)
 
     def expert_compute(rows_in):
-        both = jnp.dot(rows_in, gate_up, preferred_element_type=jnp.float32)
-        hidden = (jax.nn.silu(both[:, :hid_total]) * both[:, hid_total:]).astype(jnp.bfloat16)
-        return jnp.dot(hidden, down_all, preferred_element_type=jnp.float32).astype(jnp.bfloat16)
+        near = expert_part(rows_in, near_gate_up, near_down, near_hid)
+        far = expert_part(rows_in, far_gate_up, far_down, far_hid)
+        return (near + far).astype(jnp.bfloat16)
 
     def prepare(tokens_in, route_ids):
         x_float = tokens_in.astype(jnp.float32)

time: 392 us -> 389 us (level)
    unnamed x20 -> x49, local copies, waits for them, and re-layouts: 19.4 us -> 17.7 us
    dot_general x8 -> x16, matrix products: 46.9 us -> 45.5 us  [the longest x8 35.8 us: expert_part(): both = jnp.dot(rows_in, gate_up, preferred_element_type=jnp.float32)]
  transfers between devices with their start and end apart: 23 -> 23, of which waited for: 14 -> 14; matrix products, arithmetic and copies ran while one was open for 21% -> 20% of each run, Pallas kernels for 0% -> 0%
where the time goes in v2:
time: 389 us; the launch traced here: 388 us
  waiting for transfers between devices  232 us (60%)
  starting transfers between devices  65.2 us (17%)
  matrix products  58.1 us (15%)
  local copies, waits for them, and re-layouts  25.7 us (7%)
  other arithmetic  6.25 us (2%)
    ppermute x16, waiting for transfers between devices, passed_along(): return lax.ppermute(value, axis, pairs)  155 us
    all_to_all x4, waiting for transfers between devices, finish(): lax.all_to_all(summed.reshape(row_size, capacity, width), ROW, split_axis...  56.9 us
    dot_general x8, matrix products, expert_part(): both = jnp.dot(rows_in, gate_up, preferred_element_type=jnp.float32)  35.8 us
    ppermute x16, starting transfers between devices, passed_along(): return lax.ppermute(value, axis, pairs)  24.1 us
    all_to_all x4, starting transfers between devices, finish(): lax.all_to_all(summed.reshape(row_size, capacity, width), ROW, split_axis...  22.9 us
    all_to_all x2, waiting for transfers between devices, body(): lax.all_to_all(parts[3], ROW, split_axis=0, concat_axis=0, tiled=True)  19.7 us
    unnamed x49, local copies, waits for them, and re-layouts  17.7 us
    all_to_all x1, starting transfers between devices, body(): lax.all_to_all(stacked, ROW, split_axis=0, concat_axis=0, tiled=True)  10.1 us
  transfers between devices with their start and end apart: 23, of which 14 were waited for; matrix products, arithmetic and copies ran while one was open for 20% of the time, Pallas kernels for 0%

profile of v2, /device:TPU:1, one launch (start us, length us, event | category | flops | bytes accessed | tf_op | source)
XLA Modules:
  0.0 387.9 jit_solution(16366705829599607134)
XLA Ops:
  0.0 2.1 collective-permute-start
  2.1 1.5 collective-permute-start.1
  3.6 2.7 collective-permute-start.3
  15.4 10.1 %all-to-all-start = ((bf16[16,2,8,3584]{3,2,1,0:T(8,128)(2,1)}), bf16[16,2,8,3584]{3,2,1,0:T(8,128)(2,1)}, u32[]{:S(2)}, u32[]{:S(2)}) async-start(bf16[16,2,8,3584]{3,2,1,0:T(8,128)(2,1)} %pad_maximum_fusion.1), calls=%async_computation | async-start | bytes 3670016 | tf_op jit(solution)/shard_map/all_to_all | solution.py:87
  25.7 3.1 constant_dynamic-update-slice_fusion.5
  28.8 12.9 %collective-permute-done = bf16[3584,256]{1,0:T(8,128)(2,1)} collective-permute-done((bf16[3584,256]{1,0:T(8,128)(2,1)}, bf16[3584,256]{1,0:T(8,128)(2,1)}, u32[]{:S(2)}, u32[]{:S(2)}) %collective-permute-start) | collective-permute-done | bytes 1835040 | tf_op jit(solution)/shard_map/ppermute | solution.py:14
  41.7 3.1 collective-permute-start.5
  47.4 3.1 constant_dynamic-update-slice_fusion.4
  50.5 3.0 constant_dynamic-update-slice_fusion.3
  53.5 1.6 constant_dynamic-update-slice_fusion.2
  55.1 25.9 %collective-permute-done.2 = bf16[3584,256]{1,0:T(8,128)(2,1)} collective-permute-done((bf16[3584,256]{1,0:T(8,128)(2,1)}, bf16[3584,256]{1,0:T(8,128)(2,1)}, u32[]{:S(2)}, u32[]{:S(2)}) %collective-permute-start.2) | collective-permute-done | bytes 1835040 | tf_op jit(solution)/shard_map/ppermute | solution.py:14
  81.0 3.1 collective-permute-start.7
  84.1 3.1 constant_dynamic-update-slice_fusion.1
  88.6 31.6 %collective-permute-done.4 = bf16[256,3584]{1,0:T(8,128)(2,1)S(1)} collective-permute-done((bf16[256,3584]{1,0:T(8,128)(2,1)}, bf16[256,3584]{1,0:T(8,128)(2,1)S(1)}, u32[]{:S(2)}, u32[]{:S(2)}) %collective-permute-start.4) | collective-permute-done | bytes 1835040 | tf_op jit(solution)/shard_map/ppermute | solution.py:14
  120.2 3.1 collective-permute-start.9
  123.6 1.7 constant_dynamic-update-slice_fusion
  125.2 14.6 %collective-permute-done.6 = bf16[3584,128]{1,0:T(8,128)(2,1)S(1)} collective-permute-done((bf16[3584,128]{1,0:T(8,128)(2,1)S(1)}, bf16[3584,128]{1,0:T(8,128)(2,1)S(1)}, u32[]{:S(2)}, u32[]{:S(2)}) %collective-permute-start.6) | collective-permute-done | bytes 917536 | tf_op jit(solution)/shard_map/ppermute | solution.py:14
  139.9 3.1 collective-permute-start.11
  144.0 35.2 %collective-permute-done.10 = bf16[128,3584]{1,0:T(8,128)(2,1)S(1)} collective-permute-done((bf16[128,3584]{1,0:T(8,128)(2,1)S(1)}, bf16[128,3584]{1,0:T(8,128)(2,1)S(1)}, u32[]{:S(2)}, u32[]{:S(2)}) %collective-permute-start.10) | collective-permute-done | bytes 917536 | tf_op jit(solution)/shard_map/ppermute | solution.py:14
  182.5 3.0 fusion.56
  185.9 6.1 %fusion.57 = f32[128,1536]{1,0:T(8,128)S(1)} fusion(bf16[3584,1536]{1,0:T(8,128)(2,1)} %constant_dynamic-update-slice_fusion, bf16[16,2,8,3584]{3,2,1,0:T(8,128)(2,1)} %all-to-all-done), kind=kOutput, calls=%fused_computation.86 | convolution fusion | flops 1409286144 | bytes 12713984 | tf_op jit(solution)/shard_map/dot_general | solution.py:44
  192.1 2.0 fusion.15
  194.1 11.7 %all-to-all-start.1 = ((bf16[16,8,3584]{2,1,0:T(8,128)(2,1)}), bf16[16,8,3584]{2,1,0:T(8,128)(2,1)}, u32[]{:S(2)}, u32[]{:S(2)}) async-start(bf16[16,8,3584]{2,1,0:T(8,128)(2,1)} %fusion.15), calls=%async_computation.1 | async-start | bytes 1835008 | tf_op jit(solution)/shard_map/all_to_all | solution.py:73
  205.8 3.0 fusion.58
  209.2 6.1 %fusion.59 = f32[128,1536]{1,0:T(8,128)S(1)} fusion(bf16[3584,1536]{1,0:T(8,128)(2,1)} %constant_dynamic-update-slice_fusion, bf16[16,2,8,3584]{3,2,1,0:T(8,128)(2,1)} %all-to-all-done), kind=kOutput, calls=%fused_computation.88 | convolution fusion | flops 1409286144 | bytes 12713984 | tf_op jit(solution)/shard_map/dot_general | solution.py:44
  215.4 2.0 fusion.13
  217.3 13.9 %all-to-all-done.1 = bf16[16,8,3584]{2,1,0:T(8,128)(2,1)} async-done(((bf16[16,8,3584]{2,1,0:T(8,128)(2,1)}), bf16[16,8,3584]{2,1,0:T(8,128)(2,1)}, u32[]{:S(2)}, u32[]{:S(2)}) %all-to-all-start.1) | async-done | bytes 917536 | tf_op jit(solution)/shard_map/all_to_all | solution.py:73
  231.2 4.2 %all-to-all-start.4 = ((bf16[16,8,3584]{2,1,0:T(8,128)(2,1)}), bf16[16,8,3584]{2,1,0:T(8,128)(2,1)}, u32[]{:S(2)}, u32[]{:S(2)}) async-start(bf16[16,8,3584]{2,1,0:T(8,128)(2,1)} %fusion.13), calls=%async_computation.4 | async-start | bytes 1835008 | tf_op jit(solution)/shard_map/all_to_all | solution.py:73
  235.8 1.5 fusion.16
  238.6 12.3 %collective-permute-done.12 = bf16[64,3584]{1,0:T(8,128)(2,1)S(1)} collective-permute-done((bf16[64,3584]{1,0:T(8,128)(2,1)S(1)}, bf16[64,3584]{1,0:T(8,128)(2,1)S(1)}, u32[]{:S(2)}, u32[]{:S(2)}) %collective-permute-start.12) | collective-permute-done | bytes 458784 | tf_op jit(solution)/shard_map/ppermute | solution.py:14
  252.5 7.4 %all-to-all-done.4 = bf16[16,8,3584]{2,1,0:T(8,128)(2,1)} async-done(((bf16[16,8,3584]{2,1,0:T(8,128)(2,1)}), bf16[16,8,3584]{2,1,0:T(8,128)(2,1)}, u32[]{:S(2)}, u32[]{:S(2)}) %all-to-all-start.4) | async-done | bytes 917536 | tf_op jit(solution)/shard_map/all_to_all | solution.py:73
  259.9 3.5 all-to-all-start.2
  264.8 1.6 fusion.18
  267.7 12.2 %collective-permute-done.14 = bf16[64,3584]{1,0:T(8,128)(2,1)S(1)} collective-permute-done((bf16[64,3584]{1,0:T(8,128)(2,1)S(1)}, bf16[64,3584]{1,0:T(8,128)(2,1)S(1)}, u32[]{:S(2)}, u32[]{:S(2)}) %collective-permute-start.14) | collective-permute-done | bytes 458784 | tf_op jit(solution)/shard_map/ppermute | solution.py:14
  282.1 6.5 %all-to-all-done.2 = bf16[16,8,3584]{2,1,0:T(8,128)(2,1)S(1)} async-done(((bf16[16,8,3584]{2,1,0:T(8,128)(2,1)}), bf16[16,8,3584]{2,1,0:T(8,128)(2,1)S(1)}, u32[]{:S(2)}, u32[]{:S(2)}) %all-to-all-start.2) | async-done | bytes 917536 | tf_op jit(solution)/shard_map/all_to_all | solution.py:91
  288.6 4.4 %all-to-all-start.5 = ((bf16[16,8,3584]{2,1,0:T(8,128)(2,1)}), bf16[16,8,3584]{2,1,0:T(8,128)(2,1)}, u32[]{:S(2)}, u32[]{:S(2)}) async-start(bf16[16,8,3584]{2,1,0:T(8,128)(2,1)} %fusion.11), calls=%async_computation.5 | async-start | bytes 1835008 | tf_op jit(solution)/shard_map/all_to_all | solution.py:91
  293.0 2.7 fusion.51
  296.1 5.9 %fusion.53 = f32[128,1536]{1,0:T(8,128)S(1)} fusion(bf16[3584,1536]{1,0:T(8,128)(2,1)} %constant_dynamic-update-slice_fusion, bf16[16,8,3584]{2,1,0:T(8,128)(2,1)S(1)} %all-to-all-done.2), kind=kOutput, calls=%fused_computation.82 | convolution fusion | flops 1409286144 | bytes 12713984 | tf_op jit(solution)/shard_map/dot_general | solution.py:44
  302.0 2.0 fusion.14
  304.0 13.2 %all-to-all-done.5 = bf16[16,8,3584]{2,1,0:T(8,128)(2,1)} async-done(((bf16[16,8,3584]{2,1,0:T(8,128)(2,1)}), bf16[16,8,3584]{2,1,0:T(8,128)(2,1)}, u32[]{:S(2)}, u32[]{:S(2)}) %all-to-all-start.5) | async-done | bytes 917536 | tf_op jit(solution)/shard_map/all_to_all | solution.py:91
  317.2 3.5 all-to-all-start.3
  320.8 3.0 fusion.45
  324.2 6.1 %fusion.47 = f32[128,1536]{1,0:T(8,128)S(1)} fusion(bf16[3584,1536]{1,0:T(8,128)(2,1)} %constant_dynamic-update-slice_fusion, bf16[16,8,3584]{2,1,0:T(8,128)(2,1)} %all-to-all-done.5), kind=kOutput, calls=%fused_computation.76 | convolution fusion | flops 1409286144 | bytes 12713984 | tf_op jit(solution)/shard_map/dot_general | solution.py:44
  330.4 2.0 fusion.12
  332.3 13.6 %all-to-all-done.3 = bf16[16,8,3584]{2,1,0:T(8,128)(2,1)S(1)} async-done(((bf16[16,8,3584]{2,1,0:T(8,128)(2,1)}), bf16[16,8,3584]{2,1,0:T(8,128)(2,1)S(1)}, u32[]{:S(2)}, u32[]{:S(2)}) %all-to-all-start.3) | async-done | bytes 917536 | tf_op jit(solution)/shard_map/all_to_all | solution.py:73
  345.9 3.5 all-to-all-start.6
  352.4 22.1 %all-to-all-done.6 = bf16[16,8,3584]{2,1,0:T(8,128)(2,1)S(1)} async-done(((bf16[16,8,3584]{2,1,0:T(8,128)(2,1)}), bf16[16,8,3584]{2,1,0:T(8,128)(2,1)S(1)}, u32[]{:S(2)}, u32[]{:S(2)}) %all-to-all-start.6) | async-done | bytes 917536 | tf_op jit(solution)/shard_map/all_to_all | solution.py:73
  376.1 10.8 %collective-permute-done.15 = bf16[64,3584]{1,0:T(8,128)(2,1)S(1)} collective-permute-done((bf16[64,3584]{1,0:T(8,128)(2,1)S(1)}, bf16[64,3584]{1,0:T(8,128)(2,1)S(1)}, u32[]{:S(2)}, u32[]{:S(2)}) %collective-permute-start.15) | collective-permute-done | bytes 458784 | tf_op jit(solution)/shard_map/ppermute | solution.py:14
  (117 shorter events, 33.0 us)
Async XLA Ops:
  0.0 235.4 %copy-start = (bf16[1,3584,16]{1,2,0:T(8,128)(2,1)S(1)}, bf16[1,3584,16]{1,2,0:T(8,128)(2,1)}, u32[]{:S(2)}) copy-start(bf16[1,3584,16]{1,2,0:T(8,128)(2,1)} %param.9) | copy-start | bytes 344068
  0.0 41.7 %collective-permute-start = (bf16[3584,256]{1,0:T(8,128)(2,1)}, bf16[3584,256]{1,0:T(8,128)(2,1)}, u32[]{:S(2)}, u32[]{:S(2)}) collective-permute-start(bf16[3584,256]{1,0:T(8,128)(2,1)} %bitcast.132), channel_id=1, source_target_pairs={{0,16},{16,32},{32,48},{48,0},{1,17},{17,33},{33,49},{49,1},{2,18}... | collective-permute-start | bytes 5505032 | tf_op jit(solution)/shard_map/ppermute | solution.py:14
  2.1 43.9 %collective-permute-start.1 = (bf16[3584,256]{1,0:T(8,128)(2,1)}, bf16[3584,256]{1,0:T(8,128)(2,1)}, u32[]{:S(2)}, u32[]{:S(2)}) collective-permute-start(bf16[3584,256]{1,0:T(8,128)(2,1)} %bitcast.133), channel_id=1, source_target_pairs={{0,48},{16,0},{32,16},{48,32},{1,49},{17,1},{33,17},{49,33},{2,50}... | collective-permute-start | bytes 5505032 | tf_op jit(solution)/shard_map/ppermute | solution.py:14
  3.6 77.3 %collective-permute-start.2 = (bf16[3584,256]{1,0:T(8,128)(2,1)}, bf16[3584,256]{1,0:T(8,128)(2,1)}, u32[]{:S(2)}, u32[]{:S(2)}) collective-permute-start(bf16[3584,256]{1,0:T(8,128)(2,1)} %bitcast.134), channel_id=1, source_target_pairs={{0,16},{16,32},{32,48},{48,0},{1,17},{17,33},{33,49},{49,1},{2,18}... | collective-permute-start | bytes 5505032 | tf_op jit(solution)/shard_map/ppermute | solution.py:14
  3.6 84.8 %collective-permute-start.3 = (bf16[3584,256]{1,0:T(8,128)(2,1)}, bf16[3584,256]{1,0:T(8,128)(2,1)S(1)}, u32[]{:S(2)}, u32[]{:S(2)}) collective-permute-start(bf16[3584,256]{1,0:T(8,128)(2,1)} %bitcast.135), channel_id=1, source_target_pairs={{0,48},{16,0},{32,16},{48,32},{1,49},{17,1},{33,17},{49,33},{2,50}... | collective-permute-start | bytes 5505032 | tf_op jit(solution)/shard_map/ppermute | solution.py:14
  15.4 167.0 %all-to-all-start = ((bf16[16,2,8,3584]{3,2,1,0:T(8,128)(2,1)}), bf16[16,2,8,3584]{3,2,1,0:T(8,128)(2,1)}, u32[]{:S(2)}, u32[]{:S(2)}) async-start(bf16[16,2,8,3584]{3,2,1,0:T(8,128)(2,1)} %pad_maximum_fusion.1), calls=%async_computation | async-start | bytes 3670016 | tf_op jit(solution)/shard_map/all_to_all | solution.py:87
  25.6 16.1 %copy-start.15 = (bf16[1,1,256,3584]{3,2,1,0:T(8,128)(2,1)S(1)}, bf16[1,1,256,3584]{3,2,1,0:T(8,128)(2,1)}, u32[]{:S(2)}) copy-start(bf16[1,1,256,3584]{3,2,1,0:T(8,128)(2,1)} %param.13) | copy-start | bytes 5505028
  25.6 94.6 %collective-permute-start.4 = (bf16[256,3584]{1,0:T(8,128)(2,1)}, bf16[256,3584]{1,0:T(8,128)(2,1)S(1)}, u32[]{:S(2)}, u32[]{:S(2)}) collective-permute-start(bf16[256,3584]{1,0:T(8,128)(2,1)} %bitcast.138), channel_id=1, source_target_pairs={{0,16},{16,32},{32,48},{48,0},{1,17},{17,33},{33,49},{49,1},{2,18}... | collective-permute-start | bytes 5505032 | tf_op jit(solution)/shard_map/ppermute | solution.py:14
  41.7 81.7 %collective-permute-start.5 = (bf16[256,3584]{1,0:T(8,128)(2,1)S(1)}, bf16[256,3584]{1,0:T(8,128)(2,1)S(1)}, u32[]{:S(2)}, u32[]{:S(2)}) collective-permute-start(bf16[256,3584]{1,0:T(8,128)(2,1)S(1)} %bitcast.139), channel_id=1, source_target_pairs={{0,48},{16,0},{32,16},{48,32},{1,49},{17,1},{33,17},{49,33},{2,50}... | collective-permute-start | bytes 5505032 | tf_op jit(solution)/shard_map/ppermute | solution.py:14
  46.0 93.8 %collective-permute-start.6 = (bf16[3584,128]{1,0:T(8,128)(2,1)S(1)}, bf16[3584,128]{1,0:T(8,128)(2,1)S(1)}, u32[]{:S(2)}, u32[]{:S(2)}) collective-permute-start(bf16[3584,128]{1,0:T(8,128)(2,1)S(1)} %split.24), channel_id=1, source_target_pairs={{0,16},{16,32},{32,48},{48,0},{1,17},{17,33},{33,49},{49,1},{2,18}... | collective-permute-start | bytes 2752520 | tf_op jit(solution)/shard_map/ppermute | solution.py:14
  47.4 6.1 %copy-start.4 = (bf16[1,1,3584,256]{3,2,1,0:T(8,128)(2,1)S(1)}, bf16[1,1,3584,256]{3,2,1,0:T(8,128)(2,1)}, u32[]{:S(2)}) copy-start(bf16[1,1,3584,256]{3,2,1,0:T(8,128)(2,1)} %param.12) | copy-start | bytes 5505028
  81.0 98.3 %collective-permute-start.7 = (bf16[3584,128]{1,0:T(8,128)(2,1)S(1)}, bf16[3584,128]{1,0:T(8,128)(2,1)S(1)}, u32[]{:S(2)}, u32[]{:S(2)}) collective-permute-start(bf16[3584,128]{1,0:T(8,128)(2,1)S(1)} %split.25), channel_id=1, source_target_pairs={{0,48},{16,0},{32,16},{48,32},{1,49},{17,1},{33,17},{49,33},{2,50}... | collective-permute-start | bytes 2752520 | tf_op jit(solution)/shard_map/ppermute | solution.py:14
  88.4 91.9 %collective-permute-start.8 = (bf16[3584,128]{1,0:T(8,128)(2,1)S(1)}, bf16[3584,128]{1,0:T(8,128)(2,1)S(1)}, u32[]{:S(2)}, u32[]{:S(2)}) collective-permute-start(bf16[3584,128]{1,0:T(8,128)(2,1)S(1)} %split.26), channel_id=1, source_target_pairs={{0,16},{16,32},{32,48},{48,0},{1,17},{17,33},{33,49},{49,1},{2,18}... | collective-permute-start | bytes 2752520 | tf_op jit(solution)/shard_map/ppermute | solution.py:14
  120.2 3.2 copy-start.5
  120.2 61.2 %collective-permute-start.9 = (bf16[3584,128]{1,0:T(8,128)(2,1)S(1)}, bf16[3584,128]{1,0:T(8,128)(2,1)S(1)}, u32[]{:S(2)}, u32[]{:S(2)}) collective-permute-start(bf16[3584,128]{1,0:T(8,128)(2,1)S(1)} %split.27), channel_id=1, source_target_pairs={{0,48},{16,0},{32,16},{48,32},{1,49},{17,1},{33,17},{49,33},{2,50}... | collective-permute-start | bytes 2752520 | tf_op jit(solution)/shard_map/ppermute | solution.py:14
  123.4 20.6 %copy-start.10 = (bf16[256,3584]{1,0:T(8,128)(2,1)}, bf16[256,3584]{1,0:T(8,128)(2,1)S(1)}, u32[]{:S(2)}) copy-start(bf16[256,3584]{1,0:T(8,128)(2,1)S(1)} %collective-permute-done.5) | copy-start | bytes 5505028
  123.4 55.8 %collective-permute-start.10 = (bf16[128,3584]{1,0:T(8,128)(2,1)S(1)}, bf16[128,3584]{1,0:T(8,128)(2,1)S(1)}, u32[]{:S(2)}, u32[]{:S(2)}) collective-permute-start(bf16[128,3584]{1,0:T(8,128)(2,1)S(1)} %split.28), channel_id=1, source_target_pairs={{0,16},{16,32},{32,48},{48,0},{1,17},{17,33},{33,49},{49,1},{2,18}... | collective-permute-start | bytes 2752520 | tf_op jit(solution)/shard_map/ppermute | solution.py:14
  139.9 42.5 %collective-permute-start.11 = (bf16[128,3584]{1,0:T(8,128)(2,1)S(1)}, bf16[128,3584]{1,0:T(8,128)(2,1)S(1)}, u32[]{:S(2)}, u32[]{:S(2)}) collective-permute-start(bf16[128,3584]{1,0:T(8,128)(2,1)S(1)} %split.29), channel_id=1, source_target_pairs={{0,48},{16,0},{32,16},{48,32},{1,49},{17,1},{33,17},{49,33},{2,50}... | collective-permute-start | bytes 2752520 | tf_op jit(solution)/shard_map/ppermute | solution.py:14
  185.9 6.2 %copy-start.6 = (bf16[256,3584]{1,0:T(8,128)(2,1)S(1)}, bf16[256,3584]{1,0:T(8,128)(2,1)}, u32[]{:S(2)}) copy-start(bf16[256,3584]{1,0:T(8,128)(2,1)} %copy-done.5) | copy-start | bytes 5505028
  185.9 6.2 %copy-start.11 = (bf16[256,3584]{1,0:T(8,128)(2,1)S(1)}, bf16[256,3584]{1,0:T(8,128)(2,1)}, u32[]{:S(2)}) copy-start(bf16[256,3584]{1,0:T(8,128)(2,1)} %copy-done.10) | copy-start | bytes 5505028
  185.9 6.2 %copy-start.16 = (bf16[1,1,256,3584]{3,2,1,0:T(8,128)(2,1)S(1)}, bf16[1,1,256,3584]{3,2,1,0:T(8,128)(2,1)}, u32[]{:S(2)}) copy-start(bf16[1,1,256,3584]{3,2,1,0:T(8,128)(2,1)} %param.13) | copy-start | bytes 5505028
  194.1 37.1 %all-to-all-start.1 = ((bf16[16,8,3584]{2,1,0:T(8,128)(2,1)}), bf16[16,8,3584]{2,1,0:T(8,128)(2,1)}, u32[]{:S(2)}, u32[]{:S(2)}) async-start(bf16[16,8,3584]{2,1,0:T(8,128)(2,1)} %fusion.15), calls=%async_computation.1 | async-start | bytes 1835008 | tf_op jit(solution)/shard_map/all_to_all | solution.py:73
  209.1 6.2 %copy-start.7 = (bf16[256,3584]{1,0:T(8,128)(2,1)S(1)}, bf16[256,3584]{1,0:T(8,128)(2,1)}, u32[]{:S(2)}) copy-start(bf16[256,3584]{1,0:T(8,128)(2,1)} %copy-done.5) | copy-start | bytes 5505028
  209.2 6.2 %copy-start.12 = (bf16[256,3584]{1,0:T(8,128)(2,1)S(1)}, bf16[256,3584]{1,0:T(8,128)(2,1)}, u32[]{:S(2)}) copy-start(bf16[256,3584]{1,0:T(8,128)(2,1)} %copy-done.10) | copy-start | bytes 5505028
  209.2 6.2 %copy-start.17 = (bf16[1,1,256,3584]{3,2,1,0:T(8,128)(2,1)S(1)}, bf16[1,1,256,3584]{3,2,1,0:T(8,128)(2,1)}, u32[]{:S(2)}) copy-start(bf16[1,1,256,3584]{3,2,1,0:T(8,128)(2,1)} %param.13) | copy-start | bytes 5505028
  215.4 20.1 %copy-start.1 = (bf16[1,2,64,3584]{3,2,1,0:T(8,128)(2,1)S(1)}, bf16[1,2,64,3584]{3,2,1,0:T(8,128)(2,1)}, u32[]{:S(2)}) copy-start(bf16[1,2,64,3584]{3,2,1,0:T(8,128)(2,1)} %param.7) | copy-start | bytes 2752516
  231.2 28.7 %all-to-all-start.4 = ((bf16[16,8,3584]{2,1,0:T(8,128)(2,1)}), bf16[16,8,3584]{2,1,0:T(8,128)(2,1)}, u32[]{:S(2)}, u32[]{:S(2)}) async-start(bf16[16,8,3584]{2,1,0:T(8,128)(2,1)} %fusion.13), calls=%async_computation.4 | async-start | bytes 1835008 | tf_op jit(solution)/shard_map/all_to_all | solution.py:73
  237.3 13.6 %collective-permute-start.12 = (bf16[64,3584]{1,0:T(8,128)(2,1)S(1)}, bf16[64,3584]{1,0:T(8,128)(2,1)S(1)}, u32[]{:S(2)}, u32[]{:S(2)}) collective-permute-start(bf16[64,3584]{1,0:T(8,128)(2,1)S(1)} %fusion.16), channel_id=1, source_target_pairs={{0,64},{64,128},{128,192},{192,0},{1,65},{65,129},{129,193},{193,1... | collective-permute-start | bytes 1376264 | tf_op jit(solution)/shard_map/ppermute | solution.py:14
  259.9 28.7 %all-to-all-start.2 = ((bf16[16,8,3584]{2,1,0:T(8,128)(2,1)}), bf16[16,8,3584]{2,1,0:T(8,128)(2,1)S(1)}, u32[]{:S(2)}, u32[]{:S(2)}) async-start(bf16[16,8,3584]{2,1,0:T(8,128)(2,1)} %fusion.10), calls=%async_computation.2 | async-start | bytes 1835008 | tf_op jit(solution)/shard_map/all_to_all | solution.py:91
  266.4 13.5 %collective-permute-start.14 = (bf16[64,3584]{1,0:T(8,128)(2,1)S(1)}, bf16[64,3584]{1,0:T(8,128)(2,1)S(1)}, u32[]{:S(2)}, u32[]{:S(2)}) collective-permute-start(bf16[64,3584]{1,0:T(8,128)(2,1)S(1)} %fusion.18), channel_id=1, source_target_pairs={{0,64},{64,128},{128,192},{192,0},{1,65},{65,129},{129,193},{193,1... | collective-permute-start | bytes 1376264 | tf_op jit(solution)/shard_map/ppermute | solution.py:14
  279.9 0.8 copy-start.2
  288.6 28.7 %all-to-all-start.5 = ((bf16[16,8,3584]{2,1,0:T(8,128)(2,1)}), bf16[16,8,3584]{2,1,0:T(8,128)(2,1)}, u32[]{:S(2)}, u32[]{:S(2)}) async-start(bf16[16,8,3584]{2,1,0:T(8,128)(2,1)} %fusion.11), calls=%async_computation.5 | async-start | bytes 1835008 | tf_op jit(solution)/shard_map/all_to_all | solution.py:91
  296.1 5.9 %copy-start.8 = (bf16[256,3584]{1,0:T(8,128)(2,1)S(1)}, bf16[256,3584]{1,0:T(8,128)(2,1)}, u32[]{:S(2)}) copy-start(bf16[256,3584]{1,0:T(8,128)(2,1)} %copy-done.5) | copy-start | bytes 5505028
  296.1 5.9 %copy-start.13 = (bf16[256,3584]{1,0:T(8,128)(2,1)S(1)}, bf16[256,3584]{1,0:T(8,128)(2,1)}, u32[]{:S(2)}) copy-start(bf16[256,3584]{1,0:T(8,128)(2,1)} %copy-done.10) | copy-start | bytes 5505028
  296.1 5.9 %copy-start.18 = (bf16[1,1,256,3584]{3,2,1,0:T(8,128)(2,1)S(1)}, bf16[1,1,256,3584]{3,2,1,0:T(8,128)(2,1)}, u32[]{:S(2)}) copy-start(bf16[1,1,256,3584]{3,2,1,0:T(8,128)(2,1)} %param.13) | copy-start | bytes 5505028
  317.2 28.7 %all-to-all-start.3 = ((bf16[16,8,3584]{2,1,0:T(8,128)(2,1)}), bf16[16,8,3584]{2,1,0:T(8,128)(2,1)S(1)}, u32[]{:S(2)}, u32[]{:S(2)}) async-start(bf16[16,8,3584]{2,1,0:T(8,128)(2,1)} %fusion.14), calls=%async_computation.3 | async-start | bytes 1835008 | tf_op jit(solution)/shard_map/all_to_all | solution.py:73
  324.2 6.2 %copy-start.9 = (bf16[256,3584]{1,0:T(8,128)(2,1)S(1)}, bf16[256,3584]{1,0:T(8,128)(2,1)}, u32[]{:S(2)}) copy-start(bf16[256,3584]{1,0:T(8,128)(2,1)} %copy-done.5) | copy-start | bytes 5505028
  324.2 6.2 %copy-start.14 = (bf16[256,3584]{1,0:T(8,128)(2,1)S(1)}, bf16[256,3584]{1,0:T(8,128)(2,1)}, u32[]{:S(2)}) copy-start(bf16[256,3584]{1,0:T(8,128)(2,1)} %copy-done.10) | copy-start | bytes 5505028
  324.2 6.2 %copy-start.19 = (bf16[1,1,256,3584]{3,2,1,0:T(8,128)(2,1)S(1)}, bf16[1,1,256,3584]{3,2,1,0:T(8,128)(2,1)}, u32[]{:S(2)}) copy-start(bf16[1,1,256,3584]{3,2,1,0:T(8,128)(2,1)} %param.13) | copy-start | bytes 5505028
  330.4 19.4 %copy-start.3 = (bf16[64,3584]{1,0:T(8,128)(2,1)S(1)}, bf16[64,3584]{1,0:T(8,128)(2,1)}, u32[]{:S(2)}) copy-start(bf16[64,3584]{1,0:T(8,128)(2,1)} %copy-done.2) | copy-start | bytes 1376260
  345.9 28.6 %all-to-all-start.6 = ((bf16[16,8,3584]{2,1,0:T(8,128)(2,1)}), bf16[16,8,3584]{2,1,0:T(8,128)(2,1)S(1)}, u32[]{:S(2)}, u32[]{:S(2)}) async-start(bf16[16,8,3584]{2,1,0:T(8,128)(2,1)} %fusion.12), calls=%async_computation.6 | async-start | bytes 1835008 | tf_op jit(solution)/shard_map/all_to_all | solution.py:73
  351.2 24.9 %collective-permute-start.13 = (bf16[64,3584]{1,0:T(8,128)(2,1)}, bf16[64,3584]{1,0:T(8,128)(2,1)S(1)}, u32[]{:S(2)}, u32[]{:S(2)}) collective-permute-start(bf16[64,3584]{1,0:T(8,128)(2,1)} %fusion.17), channel_id=1, source_target_pairs={{0,64},{64,128},{128,192},{192,0},{1,65},{65,129},{129,193},{193,1... | collective-permute-start | bytes 1376264 | tf_op jit(solution)/shard_map/ppermute | solution.py:14
  374.8 12.1 %collective-permute-start.15 = (bf16[64,3584]{1,0:T(8,128)(2,1)S(1)}, bf16[64,3584]{1,0:T(8,128)(2,1)S(1)}, u32[]{:S(2)}, u32[]{:S(2)}) collective-permute-start(bf16[64,3584]{1,0:T(8,128)(2,1)S(1)} %fusion.19), channel_id=1, source_target_pairs={{0,64},{64,128},{128,192},{192,0},{1,65},{65,129},{129,193},{193,1... | collective-permute-start | bytes 1376264 | tf_op jit(solution)/shard_map/ppermute | solution.py:14

commit v3 on v2

--- a/solution.py
+++ b/solution.py
@@ -47,7 +47,8 @@
 
     def expert_compute(rows_in):
         near = expert_part(rows_in, near_gate_up, near_down, near_hid)
-        far = expert_part(rows_in, far_gate_up, far_down, far_hid)
+        far_gate_up_held, far_down_held, near = lax.optimization_barrier((far_gate_up, far_down, near))
+        far = expert_part(rows_in, far_gate_up_held, far_down_held, far_hid)
         return (near + far).astype(jnp.bfloat16)
 
     def prepare(tokens_in, route_ids):

time: 389 us -> 390 us (level)
  other arithmetic: 6.25 us -> 11 us
    ppermute x16, waiting for transfers between devices: 155 us -> 161 us  [passed_along(): return lax.ppermute(value, axis, pairs)]
    reshape x0 -> x4, other arithmetic: none -> 4.67 us  [finish(): summed.reshape(row_size, capacity, width)]
    unnamed x49 -> x27, local copies, waits for them, and re-layouts: 17.7 us -> 14.5 us
where the time goes in v3:
time: 390 us; the launch traced here: 389 us
  waiting for transfers between devices  232 us (59%)
  starting transfers between devices  64.4 us (17%)
  matrix products  58.7 us (15%)
  local copies, waits for them, and re-layouts  22.4 us (6%)
  other arithmetic  11 us (3%)
    ppermute x16, waiting for transfers between devices, passed_along(): return lax.ppermute(value, axis, pairs)  161 us
    all_to_all x4, waiting for transfers between devices, finish(): lax.all_to_all(summed.reshape(row_size, capacity, width), ROW, split_axis...  53.3 us
    dot_general x8, matrix products, expert_part(): both = jnp.dot(rows_in, gate_up, preferred_element_type=jnp.float32)  35.8 us
    all_to_all x4, starting transfers between devices, finish(): lax.all_to_all(summed.reshape(row_size, capacity, width), ROW, split_axis...  23.6 us
    ppermute x16, starting transfers between devices, passed_along(): return lax.ppermute(value, axis, pairs)  22.7 us
    all_to_all x2, waiting for transfers between devices, body(): lax.all_to_all(parts[3], ROW, split_axis=0, concat_axis=0, tiled=True)  17.9 us
    unnamed x27, local copies, waits for them, and re-layouts  14.5 us
    dot_general x8, matrix products, expert_part(): return jnp.dot(hidden, down_all, preferred_element_type=jnp.float32)  12.3 us
  transfers between devices with their start and end apart: 23, of which 14 were waited for; matrix products, arithmetic and copies ran while one was open for 20% of the time, Pallas kernels for 0%

profile of v3, /device:TPU:1, one launch (start us, length us, event | category | flops | bytes accessed | tf_op | source)
XLA Modules:
  0.0 389.1 jit_solution(13741771387797571276)
XLA Ops:
  0.0 2.1 collective-permute-start
  2.1 1.5 collective-permute-start.2
  10.8 1.5 pad_maximum_fusion.1
  12.3 10.1 %all-to-all-start = ((bf16[16,2,8,3584]{3,2,1,0:T(8,128)(2,1)}), bf16[16,2,8,3584]{3,2,1,0:T(8,128)(2,1)}, u32[]{:S(2)}, u32[]{:S(2)}) async-start(bf16[16,2,8,3584]{3,2,1,0:T(8,128)(2,1)} %pad_maximum_fusion.1), calls=%async_computation | async-start | bytes 3670016 | tf_op jit(solution)/shard_map/all_to_all | solution.py:88
  22.6 3.1 constant_dynamic-update-slice_fusion.11
  25.6 55.3 %collective-permute-done.8 = bf16[256,3584]{1,0:T(8,128)(2,1)} collective-permute-done((bf16[256,3584]{1,0:T(8,128)(2,1)}, bf16[256,3584]{1,0:T(8,128)(2,1)}, u32[]{:S(2)}, u32[]{:S(2)}) %collective-permute-start.8) | collective-permute-done | bytes 1835040 | tf_op jit(solution)/shard_map/ppermute | solution.py:14
  81.0 3.1 collective-permute-start.6
  86.7 2.7 collective-permute-start.11
  90.8 1.5 constant_dynamic-update-slice_fusion.10
  92.3 3.0 constant_dynamic-update-slice_fusion.9
  95.3 1.6 constant_dynamic-update-slice_fusion.8
  96.9 23.3 %collective-permute-done.4 = bf16[3584,256]{1,0:T(8,128)(2,1)S(1)} collective-permute-done((bf16[3584,256]{1,0:T(8,128)(2,1)}, bf16[3584,256]{1,0:T(8,128)(2,1)S(1)}, u32[]{:S(2)}, u32[]{:S(2)}) %collective-permute-start.4) | collective-permute-done | bytes 1835040 | tf_op jit(solution)/shard_map/ppermute | solution.py:14
  120.2 3.1 collective-permute-start.3
  123.3 1.6 constant_dynamic-update-slice_fusion.7
  125.1 1.5 constant_dynamic-update-slice_fusion.6
  126.6 13.2 %collective-permute-done.9 = bf16[128,3584]{1,0:T(8,128)(2,1)S(1)} collective-permute-done((bf16[128,3584]{1,0:T(8,128)(2,1)S(1)}, bf16[128,3584]{1,0:T(8,128)(2,1)S(1)}, u32[]{:S(2)}, u32[]{:S(2)}) %collective-permute-start.9) | collective-permute-done | bytes 917536 | tf_op jit(solution)/shard_map/ppermute | solution.py:14
  139.9 3.1 collective-permute-start.7
  143.0 16.5 %collective-permute-done.1 = bf16[3584,128]{1,0:T(8,128)(2,1)S(1)} collective-permute-done((bf16[3584,128]{1,0:T(8,128)(2,1)S(1)}, bf16[3584,128]{1,0:T(8,128)(2,1)S(1)}, u32[]{:S(2)}, u32[]{:S(2)}) %collective-permute-start.1) | collective-permute-done | bytes 917536 | tf_op jit(solution)/shard_map/ppermute | solution.py:14
  161.7 17.5 %collective-permute-done.5 = bf16[3584,128]{1,0:T(8,128)(2,1)S(1)} collective-permute-done((bf16[3584,128]{1,0:T(8,128)(2,1)S(1)}, bf16[3584,128]{1,0:T(8,128)(2,1)S(1)}, u32[]{:S(2)}, u32[]{:S(2)}) %collective-permute-start.5) | collective-permute-done | bytes 917536 | tf_op jit(solution)/shard_map/ppermute | solution.py:14
  181.3 6.1 %fusion.53 = f32[128,1536]{1,0:T(8,128)S(1)} fusion(bf16[3584,1536]{1,0:T(8,128)(2,1)} %constant_dynamic-update-slice_fusion.6, bf16[16,2,8,3584]{3,2,1,0:T(8,128)(2,1)} %all-to-all-done), kind=kOutput, calls=%fused_computation.82 | convolution fusion | flops 1409286144 | bytes 12713984 | tf_op jit(solution)/shard_map/dot_general | solution.py:44
  187.4 2.7 fusion.78
  190.1 3.0 fusion.52
  194.7 12.3 %all-to-all-start.1 = ((bf16[16,8,3584]{2,1,0:T(8,128)(2,1)}), bf16[16,8,3584]{2,1,0:T(8,128)(2,1)}, u32[]{:S(2)}, u32[]{:S(2)}) async-start(bf16[16,8,3584]{2,1,0:T(8,128)(2,1)} %fusion.36), calls=%async_computation.1 | async-start | bytes 1835008 | tf_op jit(solution)/shard_map/all_to_all | solution.py:74
  207.0 6.1 %fusion.55 = f32[128,1536]{1,0:T(8,128)S(1)} fusion(bf16[3584,1536]{1,0:T(8,128)(2,1)} %constant_dynamic-update-slice_fusion.6, bf16[16,2,8,3584]{3,2,1,0:T(8,128)(2,1)} %all-to-all-done), kind=kOutput, calls=%fused_computation.84 | convolution fusion | flops 1409286144 | bytes 12713984 | tf_op jit(solution)/shard_map/dot_general | solution.py:44
  213.1 2.7 fusion.82
  215.8 3.0 fusion.54
  220.4 12.1 %all-to-all-done.1 = bf16[16,8,3584]{2,1,0:T(8,128)(2,1)} async-done(((bf16[16,8,3584]{2,1,0:T(8,128)(2,1)}), bf16[16,8,3584]{2,1,0:T(8,128)(2,1)}, u32[]{:S(2)}, u32[]{:S(2)}) %all-to-all-start.1) | async-done | bytes 917536 | tf_op jit(solution)/shard_map/all_to_all | solution.py:74
  232.5 4.2 %all-to-all-start.4 = ((bf16[16,8,3584]{2,1,0:T(8,128)(2,1)}), bf16[16,8,3584]{2,1,0:T(8,128)(2,1)}, u32[]{:S(2)}, u32[]{:S(2)}) async-start(bf16[16,8,3584]{2,1,0:T(8,128)(2,1)} %fusion.38), calls=%async_computation.4 | async-start | bytes 1835008 | tf_op jit(solution)/shard_map/all_to_all | solution.py:74
  237.0 1.5 fusion.8
  239.8 12.3 %collective-permute-done.12 = bf16[64,3584]{1,0:T(8,128)(2,1)S(1)} collective-permute-done((bf16[64,3584]{1,0:T(8,128)(2,1)S(1)}, bf16[64,3584]{1,0:T(8,128)(2,1)S(1)}, u32[]{:S(2)}, u32[]{:S(2)}) %collective-permute-start.12) | collective-permute-done | bytes 458784 | tf_op jit(solution)/shard_map/ppermute | solution.py:14
  253.8 7.4 %all-to-all-done.4 = bf16[16,8,3584]{2,1,0:T(8,128)(2,1)} async-done(((bf16[16,8,3584]{2,1,0:T(8,128)(2,1)}), bf16[16,8,3584]{2,1,0:T(8,128)(2,1)}, u32[]{:S(2)}, u32[]{:S(2)}) %all-to-all-start.4) | async-done | bytes 917536 | tf_op jit(solution)/shard_map/all_to_all | solution.py:74
  261.1 3.5 all-to-all-start.2
  266.0 1.6 fusion.10
  268.9 12.2 %collective-permute-done.14 = bf16[64,3584]{1,0:T(8,128)(2,1)S(1)} collective-permute-done((bf16[64,3584]{1,0:T(8,128)(2,1)S(1)}, bf16[64,3584]{1,0:T(8,128)(2,1)S(1)}, u32[]{:S(2)}, u32[]{:S(2)}) %collective-permute-start.14) | collective-permute-done | bytes 458784 | tf_op jit(solution)/shard_map/ppermute | solution.py:14
  283.3 6.5 %all-to-all-done.2 = bf16[16,8,3584]{2,1,0:T(8,128)(2,1)S(1)} async-done(((bf16[16,8,3584]{2,1,0:T(8,128)(2,1)}), bf16[16,8,3584]{2,1,0:T(8,128)(2,1)S(1)}, u32[]{:S(2)}, u32[]{:S(2)}) %all-to-all-start.2) | async-done | bytes 917536 | tf_op jit(solution)/shard_map/all_to_all | solution.py:92
  289.8 4.4 %all-to-all-start.5 = ((bf16[16,8,3584]{2,1,0:T(8,128)(2,1)}), bf16[16,8,3584]{2,1,0:T(8,128)(2,1)}, u32[]{:S(2)}, u32[]{:S(2)}) async-start(bf16[16,8,3584]{2,1,0:T(8,128)(2,1)} %fusion.7), calls=%async_computation.5 | async-start | bytes 1835008 | tf_op jit(solution)/shard_map/all_to_all | solution.py:92
  294.2 5.8 %fusion.49 = f32[128,1536]{1,0:T(8,128)S(1)} fusion(bf16[3584,1536]{1,0:T(8,128)(2,1)} %constant_dynamic-update-slice_fusion.6, bf16[16,8,3584]{2,1,0:T(8,128)(2,1)S(1)} %all-to-all-done.2), kind=kOutput, calls=%fused_computation.78 | convolution fusion | flops 1409286144 | bytes 12713984 | tf_op jit(solution)/shard_map/dot_general | solution.py:44
  300.1 2.7 fusion.80
  302.8 2.7 fusion.47
  307.1 11.4 %all-to-all-done.5 = bf16[16,8,3584]{2,1,0:T(8,128)(2,1)} async-done(((bf16[16,8,3584]{2,1,0:T(8,128)(2,1)}), bf16[16,8,3584]{2,1,0:T(8,128)(2,1)}, u32[]{:S(2)}, u32[]{:S(2)}) %all-to-all-start.5) | async-done | bytes 917536 | tf_op jit(solution)/shard_map/all_to_all | solution.py:92
  318.5 3.5 all-to-all-start.3
  322.0 6.1 %fusion.43 = f32[128,1536]{1,0:T(8,128)S(1)} fusion(bf16[3584,1536]{1,0:T(8,128)(2,1)} %constant_dynamic-update-slice_fusion.6, bf16[16,8,3584]{2,1,0:T(8,128)(2,1)} %all-to-all-done.5), kind=kOutput, calls=%fused_computation.72 | convolution fusion | flops 1409286144 | bytes 12713984 | tf_op jit(solution)/shard_map/dot_general | solution.py:44
  328.1 2.7 fusion.84
  330.8 3.0 fusion.41
  335.4 11.8 %all-to-all-done.3 = bf16[16,8,3584]{2,1,0:T(8,128)(2,1)S(1)} async-done(((bf16[16,8,3584]{2,1,0:T(8,128)(2,1)}), bf16[16,8,3584]{2,1,0:T(8,128)(2,1)S(1)}, u32[]{:S(2)}, u32[]{:S(2)}) %all-to-all-start.3) | async-done | bytes 917536 | tf_op jit(solution)/shard_map/all_to_all | solution.py:74
  347.1 3.5 all-to-all-start.6
  353.7 22.0 %all-to-all-done.6 = bf16[16,8,3584]{2,1,0:T(8,128)(2,1)S(1)} async-done(((bf16[16,8,3584]{2,1,0:T(8,128)(2,1)}), bf16[16,8,3584]{2,1,0:T(8,128)(2,1)S(1)}, u32[]{:S(2)}, u32[]{:S(2)}) %all-to-all-start.6) | async-done | bytes 917536 | tf_op jit(solution)/shard_map/all_to_all | solution.py:74
  377.3 10.8 %collective-permute-done.15 = bf16[64,3584]{1,0:T(8,128)(2,1)S(1)} collective-permute-done((bf16[64,3584]{1,0:T(8,128)(2,1)S(1)}, bf16[64,3584]{1,0:T(8,128)(2,1)S(1)}, u32[]{:S(2)}, u32[]{:S(2)}) %collective-permute-start.15) | collective-permute-done | bytes 458784 | tf_op jit(solution)/shard_map/ppermute | solution.py:14
  (99 shorter events, 35.7 us)
Async XLA Ops:
  0.0 236.7 %copy-start = (bf16[1,3584,16]{1,2,0:T(8,128)(2,1)S(1)}, bf16[1,3584,16]{1,2,0:T(8,128)(2,1)}, u32[]{:S(2)}) copy-start(bf16[1,3584,16]{1,2,0:T(8,128)(2,1)} %param.9) | copy-start | bytes 344068
  0.0 9.8 %copy-start.1 = (bf16[1,2,64,3584]{3,2,1,0:T(8,128)(2,1)S(1)}, bf16[1,2,64,3584]{3,2,1,0:T(8,128)(2,1)}, u32[]{:S(2)}) copy-start(bf16[1,2,64,3584]{3,2,1,0:T(8,128)(2,1)} %param.7) | copy-start | bytes 2752516
  0.0 86.7 %collective-permute-start = (bf16[3584,256]{1,0:T(8,128)(2,1)}, bf16[3584,256]{1,0:T(8,128)(2,1)S(1)}, u32[]{:S(2)}, u32[]{:S(2)}) collective-permute-start(bf16[3584,256]{1,0:T(8,128)(2,1)} %bitcast.132), channel_id=1, source_target_pairs={{0,16},{16,32},{32,48},{48,0},{1,17},{17,33},{33,49},{49,1},{2,18}... | collective-permute-start | bytes 5505032 | tf_op jit(solution)/shard_map/ppermute | solution.py:14
  2.1 87.4 %collective-permute-start.2 = (bf16[3584,256]{1,0:T(8,128)(2,1)}, bf16[3584,256]{1,0:T(8,128)(2,1)}, u32[]{:S(2)}, u32[]{:S(2)}) collective-permute-start(bf16[3584,256]{1,0:T(8,128)(2,1)} %bitcast.133), channel_id=1, source_target_pairs={{0,48},{16,0},{32,16},{48,32},{1,49},{17,1},{33,17},{49,33},{2,50}... | collective-permute-start | bytes 5505032 | tf_op jit(solution)/shard_map/ppermute | solution.py:14
  3.6 81.7 %collective-permute-start.10 = (bf16[256,3584]{1,0:T(8,128)(2,1)}, bf16[256,3584]{1,0:T(8,128)(2,1)}, u32[]{:S(2)}, u32[]{:S(2)}) collective-permute-start(bf16[256,3584]{1,0:T(8,128)(2,1)} %bitcast.138), channel_id=1, source_target_pairs={{0,48},{16,0},{32,16},{48,32},{1,49},{17,1},{33,17},{49,33},{2,50}... | collective-permute-start | bytes 5505032 | tf_op jit(solution)/shard_map/ppermute | solution.py:14
  5.0 76.0 %collective-permute-start.8 = (bf16[256,3584]{1,0:T(8,128)(2,1)}, bf16[256,3584]{1,0:T(8,128)(2,1)}, u32[]{:S(2)}, u32[]{:S(2)}) collective-permute-start(bf16[256,3584]{1,0:T(8,128)(2,1)} %bitcast.139), channel_id=1, source_target_pairs={{0,16},{16,32},{32,48},{48,0},{1,17},{17,33},{33,49},{49,1},{2,18}... | collective-permute-start | bytes 5505032 | tf_op jit(solution)/shard_map/ppermute | solution.py:14
  12.3 169.0 %all-to-all-start = ((bf16[16,2,8,3584]{3,2,1,0:T(8,128)(2,1)}), bf16[16,2,8,3584]{3,2,1,0:T(8,128)(2,1)}, u32[]{:S(2)}, u32[]{:S(2)}) async-start(bf16[16,2,8,3584]{3,2,1,0:T(8,128)(2,1)} %pad_maximum_fusion.1), calls=%async_computation | async-start | bytes 3670016 | tf_op jit(solution)/shard_map/all_to_all | solution.py:88
  22.4 58.6 %copy-start.4 = (bf16[1,1,3584,256]{3,2,1,0:T(8,128)(2,1)S(1)}, bf16[1,1,3584,256]{3,2,1,0:T(8,128)(2,1)}, u32[]{:S(2)}) copy-start(bf16[1,1,3584,256]{3,2,1,0:T(8,128)(2,1)} %param.12) | copy-start | bytes 5505028
  22.4 97.8 %collective-permute-start.4 = (bf16[3584,256]{1,0:T(8,128)(2,1)}, bf16[3584,256]{1,0:T(8,128)(2,1)S(1)}, u32[]{:S(2)}, u32[]{:S(2)}) collective-permute-start(bf16[3584,256]{1,0:T(8,128)(2,1)} %bitcast.134), channel_id=1, source_target_pairs={{0,16},{16,32},{32,48},{48,0},{1,17},{17,33},{33,49},{49,1},{2,18}... | collective-permute-start | bytes 5505032 | tf_op jit(solution)/shard_map/ppermute | solution.py:14
  81.0 44.0 %collective-permute-start.6 = (bf16[3584,256]{1,0:T(8,128)(2,1)S(1)}, bf16[3584,256]{1,0:T(8,128)(2,1)S(1)}, u32[]{:S(2)}, u32[]{:S(2)}) collective-permute-start(bf16[3584,256]{1,0:T(8,128)(2,1)S(1)} %bitcast.135), channel_id=1, source_target_pairs={{0,48},{16,0},{32,16},{48,32},{1,49},{17,1},{33,17},{49,33},{2,50}... | collective-permute-start | bytes 5505032 | tf_op jit(solution)/shard_map/ppermute | solution.py:14
  85.3 54.5 %collective-permute-start.9 = (bf16[128,3584]{1,0:T(8,128)(2,1)S(1)}, bf16[128,3584]{1,0:T(8,128)(2,1)S(1)}, u32[]{:S(2)}, u32[]{:S(2)}) collective-permute-start(bf16[128,3584]{1,0:T(8,128)(2,1)S(1)} %split.28), channel_id=1, source_target_pairs={{0,16},{16,32},{32,48},{48,0},{1,17},{17,33},{33,49},{49,1},{2,18}... | collective-permute-start | bytes 2752520 | tf_op jit(solution)/shard_map/ppermute | solution.py:14
  86.7 73.9 %collective-permute-start.11 = (bf16[128,3584]{1,0:T(8,128)(2,1)S(1)}, bf16[128,3584]{1,0:T(8,128)(2,1)S(1)}, u32[]{:S(2)}, u32[]{:S(2)}) collective-permute-start(bf16[128,3584]{1,0:T(8,128)(2,1)S(1)} %split.29), channel_id=1, source_target_pairs={{0,48},{16,0},{32,16},{48,32},{1,49},{17,1},{33,17},{49,33},{2,50}... | collective-permute-start | bytes 2752520 | tf_op jit(solution)/shard_map/ppermute | solution.py:14
  89.5 70.0 %collective-permute-start.1 = (bf16[3584,128]{1,0:T(8,128)(2,1)S(1)}, bf16[3584,128]{1,0:T(8,128)(2,1)S(1)}, u32[]{:S(2)}, u32[]{:S(2)}) collective-permute-start(bf16[3584,128]{1,0:T(8,128)(2,1)S(1)} %split.24), channel_id=1, source_target_pairs={{0,16},{16,32},{32,48},{48,0},{1,17},{17,33},{33,49},{49,1},{2,18}... | collective-permute-start | bytes 2752520 | tf_op jit(solution)/shard_map/ppermute | solution.py:14
  120.2 40.4 %collective-permute-start.3 = (bf16[3584,128]{1,0:T(8,128)(2,1)S(1)}, bf16[3584,128]{1,0:T(8,128)(2,1)S(1)}, u32[]{:S(2)}, u32[]{:S(2)}) collective-permute-start(bf16[3584,128]{1,0:T(8,128)(2,1)S(1)} %split.25), channel_id=1, source_target_pairs={{0,48},{16,0},{32,16},{48,32},{1,49},{17,1},{33,17},{49,33},{2,50}... | collective-permute-start | bytes 2752520 | tf_op jit(solution)/shard_map/ppermute | solution.py:14
  125.0 54.2 %collective-permute-start.5 = (bf16[3584,128]{1,0:T(8,128)(2,1)S(1)}, bf16[3584,128]{1,0:T(8,128)(2,1)S(1)}, u32[]{:S(2)}, u32[]{:S(2)}) collective-permute-start(bf16[3584,128]{1,0:T(8,128)(2,1)S(1)} %split.26), channel_id=1, source_target_pairs={{0,16},{16,32},{32,48},{48,0},{1,17},{17,33},{33,49},{49,1},{2,18}... | collective-permute-start | bytes 2752520 | tf_op jit(solution)/shard_map/ppermute | solution.py:14
  139.9 40.4 %collective-permute-start.7 = (bf16[3584,128]{1,0:T(8,128)(2,1)S(1)}, bf16[3584,128]{1,0:T(8,128)(2,1)S(1)}, u32[]{:S(2)}, u32[]{:S(2)}) collective-permute-start(bf16[3584,128]{1,0:T(8,128)(2,1)S(1)} %split.27), channel_id=1, source_target_pairs={{0,48},{16,0},{32,16},{48,32},{1,49},{17,1},{33,17},{49,33},{2,50}... | collective-permute-start | bytes 2752520 | tf_op jit(solution)/shard_map/ppermute | solution.py:14
  181.3 6.1 %copy-start.5 = (bf16[1,1,256,3584]{3,2,1,0:T(8,128)(2,1)S(1)}, bf16[1,1,256,3584]{3,2,1,0:T(8,128)(2,1)}, u32[]{:S(2)}) copy-start(bf16[1,1,256,3584]{3,2,1,0:T(8,128)(2,1)} %param.13) | copy-start | bytes 5505028
  194.7 37.8 %all-to-all-start.1 = ((bf16[16,8,3584]{2,1,0:T(8,128)(2,1)}), bf16[16,8,3584]{2,1,0:T(8,128)(2,1)}, u32[]{:S(2)}, u32[]{:S(2)}) async-start(bf16[16,8,3584]{2,1,0:T(8,128)(2,1)} %fusion.36), calls=%async_computation.1 | async-start | bytes 1835008 | tf_op jit(solution)/shard_map/all_to_all | solution.py:74
  207.0 6.1 %copy-start.6 = (bf16[1,1,256,3584]{3,2,1,0:T(8,128)(2,1)S(1)}, bf16[1,1,256,3584]{3,2,1,0:T(8,128)(2,1)}, u32[]{:S(2)}) copy-start(bf16[1,1,256,3584]{3,2,1,0:T(8,128)(2,1)} %param.13) | copy-start | bytes 5505028
  232.5 28.7 %all-to-all-start.4 = ((bf16[16,8,3584]{2,1,0:T(8,128)(2,1)}), bf16[16,8,3584]{2,1,0:T(8,128)(2,1)}, u32[]{:S(2)}, u32[]{:S(2)}) async-start(bf16[16,8,3584]{2,1,0:T(8,128)(2,1)} %fusion.38), calls=%async_computation.4 | async-start | bytes 1835008 | tf_op jit(solution)/shard_map/all_to_all | solution.py:74
  238.6 13.6 %collective-permute-start.12 = (bf16[64,3584]{1,0:T(8,128)(2,1)S(1)}, bf16[64,3584]{1,0:T(8,128)(2,1)S(1)}, u32[]{:S(2)}, u32[]{:S(2)}) collective-permute-start(bf16[64,3584]{1,0:T(8,128)(2,1)S(1)} %fusion.8), channel_id=1, source_target_pairs={{0,64},{64,128},{128,192},{192,0},{1,65},{65,129},{129,193},{193,1... | collective-permute-start | bytes 1376264 | tf_op jit(solution)/shard_map/ppermute | solution.py:14
  261.1 28.7 %all-to-all-start.2 = ((bf16[16,8,3584]{2,1,0:T(8,128)(2,1)}), bf16[16,8,3584]{2,1,0:T(8,128)(2,1)S(1)}, u32[]{:S(2)}, u32[]{:S(2)}) async-start(bf16[16,8,3584]{2,1,0:T(8,128)(2,1)} %fusion.6), calls=%async_computation.2 | async-start | bytes 1835008 | tf_op jit(solution)/shard_map/all_to_all | solution.py:92
  267.7 13.5 %collective-permute-start.14 = (bf16[64,3584]{1,0:T(8,128)(2,1)S(1)}, bf16[64,3584]{1,0:T(8,128)(2,1)S(1)}, u32[]{:S(2)}, u32[]{:S(2)}) collective-permute-start(bf16[64,3584]{1,0:T(8,128)(2,1)S(1)} %fusion.10), channel_id=1, source_target_pairs={{0,64},{64,128},{128,192},{192,0},{1,65},{65,129},{129,193},{193,1... | collective-permute-start | bytes 1376264 | tf_op jit(solution)/shard_map/ppermute | solution.py:14
  281.1 0.8 copy-start.2
  289.8 28.7 %all-to-all-start.5 = ((bf16[16,8,3584]{2,1,0:T(8,128)(2,1)}), bf16[16,8,3584]{2,1,0:T(8,128)(2,1)}, u32[]{:S(2)}, u32[]{:S(2)}) async-start(bf16[16,8,3584]{2,1,0:T(8,128)(2,1)} %fusion.7), calls=%async_computation.5 | async-start | bytes 1835008 | tf_op jit(solution)/shard_map/all_to_all | solution.py:92
  294.2 5.9 %copy-start.7 = (bf16[1,1,256,3584]{3,2,1,0:T(8,128)(2,1)S(1)}, bf16[1,1,256,3584]{3,2,1,0:T(8,128)(2,1)}, u32[]{:S(2)}) copy-start(bf16[1,1,256,3584]{3,2,1,0:T(8,128)(2,1)} %param.13) | copy-start | bytes 5505028
  318.5 28.7 %all-to-all-start.3 = ((bf16[16,8,3584]{2,1,0:T(8,128)(2,1)}), bf16[16,8,3584]{2,1,0:T(8,128)(2,1)S(1)}, u32[]{:S(2)}, u32[]{:S(2)}) async-start(bf16[16,8,3584]{2,1,0:T(8,128)(2,1)} %fusion.37), calls=%async_computation.3 | async-start | bytes 1835008 | tf_op jit(solution)/shard_map/all_to_all | solution.py:74
  322.0 6.1 %copy-start.8 = (bf16[1,1,256,3584]{3,2,1,0:T(8,128)(2,1)S(1)}, bf16[1,1,256,3584]{3,2,1,0:T(8,128)(2,1)}, u32[]{:S(2)}) copy-start(bf16[1,1,256,3584]{3,2,1,0:T(8,128)(2,1)} %param.13) | copy-start | bytes 5505028
  335.4 15.6 %copy-start.3 = (bf16[64,3584]{1,0:T(8,128)(2,1)S(1)}, bf16[64,3584]{1,0:T(8,128)(2,1)}, u32[]{:S(2)}) copy-start(bf16[64,3584]{1,0:T(8,128)(2,1)} %copy-done.2) | copy-start | bytes 1376260
  347.1 28.6 %all-to-all-start.6 = ((bf16[16,8,3584]{2,1,0:T(8,128)(2,1)}), bf16[16,8,3584]{2,1,0:T(8,128)(2,1)S(1)}, u32[]{:S(2)}, u32[]{:S(2)}) async-start(bf16[16,8,3584]{2,1,0:T(8,128)(2,1)} %fusion.39), calls=%async_computation.6 | async-start | bytes 1835008 | tf_op jit(solution)/shard_map/all_to_all | solution.py:74
  352.5 24.9 %collective-permute-start.13 = (bf16[64,3584]{1,0:T(8,128)(2,1)}, bf16[64,3584]{1,0:T(8,128)(2,1)S(1)}, u32[]{:S(2)}, u32[]{:S(2)}) collective-permute-start(bf16[64,3584]{1,0:T(8,128)(2,1)} %fusion.9), channel_id=1, source_target_pairs={{0,64},{64,128},{128,192},{192,0},{1,65},{65,129},{129,193},{193,1... | collective-permute-start | bytes 1376264 | tf_op jit(solution)/shard_map/ppermute | solution.py:14
  376.0 12.1 %collective-permute-start.15 = (bf16[64,3584]{1,0:T(8,128)(2,1)S(1)}, bf16[64,3584]{1,0:T(8,128)(2,1)S(1)}, u32[]{:S(2)}, u32[]{:S(2)}) collective-permute-start(bf16[64,3584]{1,0:T(8,128)(2,1)S(1)} %fusion.11), channel_id=1, source_target_pairs={{0,64},{64,128},{128,192},{192,0},{1,65},{65,129},{129,193},{193,1... | collective-permute-start | bytes 1376264 | tf_op jit(solution)/shard_map/ppermute | solution.py:14

commit v4 on v2

--- a/solution.py
+++ b/solution.py
@@ -68,14 +68,21 @@
         outbox = jnp.dot(placing, normed, preferred_element_type=jnp.float32).astype(jnp.bfloat16)
         return x_float, gate_val, placing, outbox.reshape(row_size, capacity, width)
 
-    def finish(arrived, x_float, gate_val, placing):
-        summed = expert_compute(arrived.reshape(-1, width))
+    def returned(summed):
         back = lax.all_to_all(
             summed.reshape(row_size, capacity, width), ROW, split_axis=0, concat_axis=0, tiled=True
         )
-        picked = jnp.dot(
-            placing.T, back.reshape(experts_here * capacity, width), preferred_element_type=jnp.float32
-        )
+        return back.reshape(experts_here * capacity, width)
+
+    def finish(arrived, x_float, gate_val, placing, split_return):
+        rows_in = arrived.reshape(-1, width)
+        if split_return:
+            near = expert_part(rows_in, near_gate_up, near_down, near_hid).astype(jnp.bfloat16)
+            far = expert_part(rows_in, far_gate_up, far_down, far_hid).astype(jnp.bfloat16)
+            back = returned(near).astype(jnp.float32) + returned(far).astype(jnp.float32)
+        else:
+            back = returned(expert_compute(rows_in))
+        picked = jnp.dot(placing.T, back, preferred_element_type=jnp.float32)
         return (x_float + gate_val[:, None] * picked).astype(jnp.bfloat16)
 
     micro_count = acts.shape[1]
@@ -92,7 +99,7 @@
                 for parts in ready
             ]
         carried = [
-            passed_along(finish(arrivals[m], *ready[m][:3]), "section", 1)
+            passed_along(finish(arrivals[m], *ready[m][:3], round_idx == 0), "section", 1)
             for m in range(micro_count)
         ]
     return jnp.stack(carried)[None]

time: 389 us -> 441 us (1.13)
  waiting for transfers between devices: 232 us -> 269 us
  starting transfers between devices: 65.2 us -> 73.4 us
  local copies, waits for them, and re-layouts: 25.7 us -> 31.8 us
    all_to_all x4 -> x6, waiting for transfers between devices: 56.9 us -> 94.5 us  [returned(): lax.all_to_all(summed.reshape(row_size, capacity, width), ROW, split_axis...]
    all_to_all x4 -> x6, starting transfers between devices: 22.9 us -> 31.3 us  [returned(): lax.all_to_all(summed.reshape(row_size, capacity, width), ROW, split_axis...]
    unnamed x49 -> x47, local copies, waits for them, and re-layouts: 17.7 us -> 17.1 us
  transfers between devices with their start and end apart: 23 -> 25, of which waited for: 14 -> 16; matrix products, arithmetic and copies ran while one was open for 20% -> 22% of each run, Pallas kernels for 0% -> 0%
where the time goes in v4:
time: 441 us; the launch traced here: 440 us
  waiting for transfers between devices  269 us (61%)
  starting transfers between devices  73.4 us (17%)
  matrix products  58.6 us (13%)
  local copies, waits for them, and re-layouts  31.8 us (7%)
  other arithmetic  6.25 us (1%)
    ppermute x16, waiting for transfers between devices, passed_along(): return lax.ppermute(value, axis, pairs)  155 us
    all_to_all x6, waiting for transfers between devices, returned(): lax.all_to_all(summed.reshape(row_size, capacity, width), ROW, split_axis...  94.5 us
    dot_general x8, matrix products, expert_part(): both = jnp.dot(rows_in, gate_up, preferred_element_type=jnp.float32)  35.9 us
    all_to_all x6, starting transfers between devices, returned(): lax.all_to_all(summed.reshape(row_size, capacity, width), ROW, split_axis...  31.3 us
    ppermute x16, starting transfers between devices, passed_along(): return lax.ppermute(value, axis, pairs)  24 us
    all_to_all x2, waiting for transfers between devices, body(): lax.all_to_all(parts[3], ROW, split_axis=0, concat_axis=0, tiled=True)  19.4 us
    unnamed x47, local copies, waits for them, and re-layouts  17.1 us
    dot_general x8, matrix products, expert_part(): return jnp.dot(hidden, down_all, preferred_element_type=jnp.float32)  11.5 us
  transfers between devices with their start and end apart: 25, of which 16 were waited for; matrix products, arithmetic and copies ran while one was open for 22% of the time, Pallas kernels for 0%

profile of v4, /device:TPU:1, one launch (start us, length us, event | category | flops | bytes accessed | tf_op | source)
XLA Modules:
  0.0 439.7 jit_solution(15770003599519114071)
XLA Ops:
  0.0 2.1 collective-permute-start
  3.7 2.7 collective-permute-start.3
  13.4 10.1 %all-to-all-start = ((bf16[16,2,8,3584]{3,2,1,0:T(8,128)(2,1)}), bf16[16,2,8,3584]{3,2,1,0:T(8,128)(2,1)}, u32[]{:S(2)}, u32[]{:S(2)}) async-start(bf16[16,2,8,3584]{3,2,1,0:T(8,128)(2,1)} %pad_maximum_fusion.1), calls=%async_computation | async-start | bytes 3670016 | tf_op jit(solution)/shard_map/all_to_all | solution.py:94
  23.6 18.1 %collective-permute-done = bf16[3584,256]{1,0:T(8,128)(2,1)} collective-permute-done((bf16[3584,256]{1,0:T(8,128)(2,1)}, bf16[3584,256]{1,0:T(8,128)(2,1)}, u32[]{:S(2)}, u32[]{:S(2)}) %collective-permute-start) | collective-permute-done | bytes 1835040 | tf_op jit(solution)/shard_map/ppermute | solution.py:14
  41.7 3.1 collective-permute-start.5
  44.8 3.0 constant_dynamic-update-slice_fusion.5
  49.0 3.0 constant_dynamic-update-slice_fusion.4
  52.0 3.0 constant_dynamic-update-slice_fusion.3
  56.2 24.7 %collective-permute-done.2 = bf16[3584,256]{1,0:T(8,128)(2,1)S(1)} collective-permute-done((bf16[3584,256]{1,0:T(8,128)(2,1)}, bf16[3584,256]{1,0:T(8,128)(2,1)S(1)}, u32[]{:S(2)}, u32[]{:S(2)}) %collective-permute-start.2) | collective-permute-done | bytes 1835040 | tf_op jit(solution)/shard_map/ppermute | solution.py:14
  80.9 3.2 collective-permute-start.7
  85.2 2.2 split.27
  87.4 32.8 %collective-permute-done.4 = bf16[256,3584]{1,0:T(8,128)(2,1)S(1)} collective-permute-done((bf16[256,3584]{1,0:T(8,128)(2,1)}, bf16[256,3584]{1,0:T(8,128)(2,1)S(1)}, u32[]{:S(2)}, u32[]{:S(2)}) %collective-permute-start.4) | collective-permute-done | bytes 1835040 | tf_op jit(solution)/shard_map/ppermute | solution.py:14
  120.2 3.1 collective-permute-start.9
  127.8 3.0 constant_dynamic-update-slice_fusion
  130.8 9.1 %collective-permute-done.6 = bf16[3584,128]{1,0:T(8,128)(2,1)S(1)} collective-permute-done((bf16[3584,128]{1,0:T(8,128)(2,1)S(1)}, bf16[3584,128]{1,0:T(8,128)(2,1)S(1)}, u32[]{:S(2)}, u32[]{:S(2)}) %collective-permute-start.6) | collective-permute-done | bytes 917536 | tf_op jit(solution)/shard_map/ppermute | solution.py:14
  139.9 3.1 collective-permute-start.11
  144.0 35.2 %collective-permute-done.10 = bf16[128,3584]{1,0:T(8,128)(2,1)S(1)} collective-permute-done((bf16[128,3584]{1,0:T(8,128)(2,1)S(1)}, bf16[128,3584]{1,0:T(8,128)(2,1)S(1)}, u32[]{:S(2)}, u32[]{:S(2)}) %collective-permute-start.10) | collective-permute-done | bytes 917536 | tf_op jit(solution)/shard_map/ppermute | solution.py:14
  180.3 6.1 %fusion.63 = f32[128,1536]{1,0:T(8,128)S(1)} fusion(bf16[3584,1536]{1,0:T(8,128)(2,1)} %constant_dynamic-update-slice_fusion, bf16[16,2,8,3584]{3,2,1,0:T(8,128)(2,1)} %all-to-all-done), kind=kOutput, calls=%fused_computation.94 | convolution fusion | flops 1409286144 | bytes 12713984 | tf_op jit(solution)/shard_map/dot_general | solution.py:44
  186.5 2.0 fusion.12
  188.5 11.6 %all-to-all-start.1 = ((bf16[16,8,3584]{2,1,0:T(8,128)(2,1)}), bf16[16,8,3584]{2,1,0:T(8,128)(2,1)}, u32[]{:S(2)}, u32[]{:S(2)}) async-start(bf16[16,8,3584]{2,1,0:T(8,128)(2,1)} %fusion.12), calls=%async_computation.1 | async-start | bytes 1835008 | tf_op jit(solution)/shard_map/all_to_all | solution.py:72
  200.1 2.2 constant_dynamic-update-slice_fusion.7
  202.4 2.2 constant_dynamic-update-slice_fusion.6
  205.8 3.0 fusion.62
  210.2 15.4 %all-to-all-done.1 = bf16[16,8,3584]{2,1,0:T(8,128)(2,1)} async-done(((bf16[16,8,3584]{2,1,0:T(8,128)(2,1)}), bf16[16,8,3584]{2,1,0:T(8,128)(2,1)}, u32[]{:S(2)}, u32[]{:S(2)}) %all-to-all-start.1) | async-done | bytes 917536 | tf_op jit(solution)/shard_map/all_to_all | solution.py:72
  225.6 4.2 all-to-all-start.2
  229.8 6.1 %fusion.65 = f32[128,1536]{1,0:T(8,128)S(1)} fusion(bf16[3584,1536]{1,0:T(8,128)(2,1)} %constant_dynamic-update-slice_fusion, bf16[16,2,8,3584]{3,2,1,0:T(8,128)(2,1)} %all-to-all-done), kind=kOutput, calls=%fused_computation.96 | convolution fusion | flops 1409286144 | bytes 12713984 | tf_op jit(solution)/shard_map/dot_general | solution.py:44
  238.0 16.3 %all-to-all-done.2 = bf16[16,8,3584]{2,1,0:T(8,128)(2,1)} async-done(((bf16[16,8,3584]{2,1,0:T(8,128)(2,1)}), bf16[16,8,3584]{2,1,0:T(8,128)(2,1)}, u32[]{:S(2)}, u32[]{:S(2)}) %all-to-all-start.2) | async-done | bytes 917536 | tf_op jit(solution)/shard_map/all_to_all | solution.py:72
  254.2 4.2 all-to-all-start.5
  258.5 3.0 fusion.64
  262.8 20.2 %all-to-all-done.5 = bf16[16,8,3584]{2,1,0:T(8,128)(2,1)} async-done(((bf16[16,8,3584]{2,1,0:T(8,128)(2,1)}), bf16[16,8,3584]{2,1,0:T(8,128)(2,1)}, u32[]{:S(2)}, u32[]{:S(2)}) %all-to-all-start.5) | async-done | bytes 917536 | tf_op jit(solution)/shard_map/all_to_all | solution.py:72
  283.0 4.2 all-to-all-start.6
  290.7 12.4 %collective-permute-done.12 = bf16[64,3584]{1,0:T(8,128)(2,1)S(1)} collective-permute-done((bf16[64,3584]{1,0:T(8,128)(2,1)S(1)}, bf16[64,3584]{1,0:T(8,128)(2,1)S(1)}, u32[]{:S(2)}, u32[]{:S(2)}) %collective-permute-start.12) | collective-permute-done | bytes 458784 | tf_op jit(solution)/shard_map/ppermute | solution.py:14
  304.7 7.0 %all-to-all-done.6 = bf16[16,8,3584]{2,1,0:T(8,128)(2,1)} async-done(((bf16[16,8,3584]{2,1,0:T(8,128)(2,1)}), bf16[16,8,3584]{2,1,0:T(8,128)(2,1)}, u32[]{:S(2)}, u32[]{:S(2)}) %all-to-all-start.6) | async-done | bytes 917536 | tf_op jit(solution)/shard_map/all_to_all | solution.py:72
  311.7 3.5 all-to-all-start.3
  319.8 12.2 %collective-permute-done.14 = bf16[64,3584]{1,0:T(8,128)(2,1)S(1)} collective-permute-done((bf16[64,3584]{1,0:T(8,128)(2,1)S(1)}, bf16[64,3584]{1,0:T(8,128)(2,1)S(1)}, u32[]{:S(2)}, u32[]{:S(2)}) %collective-permute-start.14) | collective-permute-done | bytes 458784 | tf_op jit(solution)/shard_map/ppermute | solution.py:14
  334.2 6.2 %all-to-all-done.3 = bf16[16,8,3584]{2,1,0:T(8,128)(2,1)S(1)} async-done(((bf16[16,8,3584]{2,1,0:T(8,128)(2,1)}), bf16[16,8,3584]{2,1,0:T(8,128)(2,1)S(1)}, u32[]{:S(2)}, u32[]{:S(2)}) %all-to-all-start.3) | async-done | bytes 917536 | tf_op jit(solution)/shard_map/all_to_all | solution.py:98
  340.4 4.4 %all-to-all-start.7 = ((bf16[16,8,3584]{2,1,0:T(8,128)(2,1)}), bf16[16,8,3584]{2,1,0:T(8,128)(2,1)}, u32[]{:S(2)}, u32[]{:S(2)}) async-start(bf16[16,8,3584]{2,1,0:T(8,128)(2,1)} %fusion.9), calls=%async_computation.7 | async-start | bytes 1835008 | tf_op jit(solution)/shard_map/all_to_all | solution.py:98
  344.8 2.7 fusion.58
  348.0 5.9 %fusion.60 = f32[128,1536]{1,0:T(8,128)S(1)} fusion(bf16[3584,1536]{1,0:T(8,128)(2,1)} %constant_dynamic-update-slice_fusion, bf16[16,8,3584]{2,1,0:T(8,128)(2,1)S(1)} %all-to-all-done.3), kind=kOutput, calls=%fused_computation.91 | convolution fusion | flops 1409286144 | bytes 12713984 | tf_op jit(solution)/shard_map/dot_general | solution.py:44
  353.9 2.0 fusion.11
  355.9 13.2 %all-to-all-done.7 = bf16[16,8,3584]{2,1,0:T(8,128)(2,1)} async-done(((bf16[16,8,3584]{2,1,0:T(8,128)(2,1)}), bf16[16,8,3584]{2,1,0:T(8,128)(2,1)}, u32[]{:S(2)}, u32[]{:S(2)}) %all-to-all-start.7) | async-done | bytes 917536 | tf_op jit(solution)/shard_map/all_to_all | solution.py:98
  369.0 3.5 all-to-all-start.4
  372.6 3.0 fusion.53
  376.0 6.1 %fusion.55 = f32[128,1536]{1,0:T(8,128)S(1)} fusion(bf16[3584,1536]{1,0:T(8,128)(2,1)} %constant_dynamic-update-slice_fusion, bf16[16,8,3584]{2,1,0:T(8,128)(2,1)} %all-to-all-done.7), kind=kOutput, calls=%fused_computation.86 | convolution fusion | flops 1409286144 | bytes 12713984 | tf_op jit(solution)/shard_map/dot_general | solution.py:44
  384.1 13.6 %all-to-all-done.4 = bf16[16,8,3584]{2,1,0:T(8,128)(2,1)S(1)} async-done(((bf16[16,8,3584]{2,1,0:T(8,128)(2,1)}), bf16[16,8,3584]{2,1,0:T(8,128)(2,1)S(1)}, u32[]{:S(2)}, u32[]{:S(2)}) %all-to-all-start.4) | async-done | bytes 917536 | tf_op jit(solution)/shard_map/all_to_all | solution.py:72
  397.7 3.5 all-to-all-start.8
  404.3 22.0 %all-to-all-done.8 = bf16[16,8,3584]{2,1,0:T(8,128)(2,1)S(1)} async-done(((bf16[16,8,3584]{2,1,0:T(8,128)(2,1)}), bf16[16,8,3584]{2,1,0:T(8,128)(2,1)S(1)}, u32[]{:S(2)}, u32[]{:S(2)}) %all-to-all-start.8) | async-done | bytes 917536 | tf_op jit(solution)/shard_map/all_to_all | solution.py:72
  427.9 10.8 %collective-permute-done.15 = bf16[64,3584]{1,0:T(8,128)(2,1)S(1)} collective-permute-done((bf16[64,3584]{1,0:T(8,128)(2,1)S(1)}, bf16[64,3584]{1,0:T(8,128)(2,1)S(1)}, u32[]{:S(2)}, u32[]{:S(2)}) %collective-permute-start.15) | collective-permute-done | bytes 458784 | tf_op jit(solution)/shard_map/ppermute | solution.py:14
  (119 shorter events, 45.0 us)
Async XLA Ops:
  0.0 287.2 %copy-start = (bf16[1,3584,16]{1,2,0:T(8,128)(2,1)S(1)}, bf16[1,3584,16]{1,2,0:T(8,128)(2,1)}, u32[]{:S(2)}) copy-start(bf16[1,3584,16]{1,2,0:T(8,128)(2,1)} %param.9) | copy-start | bytes 344068
  0.0 11.1 %copy-start.1 = (bf16[1,2,64,3584]{3,2,1,0:T(8,128)(2,1)S(1)}, bf16[1,2,64,3584]{3,2,1,0:T(8,128)(2,1)}, u32[]{:S(2)}) copy-start(bf16[1,2,64,3584]{3,2,1,0:T(8,128)(2,1)} %param.7) | copy-start | bytes 2752516
  0.0 41.7 %collective-permute-start = (bf16[3584,256]{1,0:T(8,128)(2,1)}, bf16[3584,256]{1,0:T(8,128)(2,1)}, u32[]{:S(2)}, u32[]{:S(2)}) collective-permute-start(bf16[3584,256]{1,0:T(8,128)(2,1)} %bitcast.136), channel_id=1, source_target_pairs={{0,16},{16,32},{32,48},{48,0},{1,17},{17,33},{33,49},{49,1},{2,18}... | collective-permute-start | bytes 5505032 | tf_op jit(solution)/shard_map/ppermute | solution.py:14
  2.1 49.8 %collective-permute-start.1 = (bf16[3584,256]{1,0:T(8,128)(2,1)}, bf16[3584,256]{1,0:T(8,128)(2,1)}, u32[]{:S(2)}, u32[]{:S(2)}) collective-permute-start(bf16[3584,256]{1,0:T(8,128)(2,1)} %bitcast.137), channel_id=1, source_target_pairs={{0,48},{16,0},{32,16},{48,32},{1,49},{17,1},{33,17},{49,33},{2,50}... | collective-permute-start | bytes 5505032 | tf_op jit(solution)/shard_map/ppermute | solution.py:14
  3.6 77.2 %collective-permute-start.2 = (bf16[3584,256]{1,0:T(8,128)(2,1)}, bf16[3584,256]{1,0:T(8,128)(2,1)S(1)}, u32[]{:S(2)}, u32[]{:S(2)}) collective-permute-start(bf16[3584,256]{1,0:T(8,128)(2,1)} %bitcast.138), channel_id=1, source_target_pairs={{0,16},{16,32},{32,48},{48,0},{1,17},{17,33},{33,49},{49,1},{2,18}... | collective-permute-start | bytes 5505032 | tf_op jit(solution)/shard_map/ppermute | solution.py:14
  3.7 81.5 %collective-permute-start.3 = (bf16[3584,256]{1,0:T(8,128)(2,1)}, bf16[3584,256]{1,0:T(8,128)(2,1)}, u32[]{:S(2)}, u32[]{:S(2)}) collective-permute-start(bf16[3584,256]{1,0:T(8,128)(2,1)} %bitcast.139), channel_id=1, source_target_pairs={{0,48},{16,0},{32,16},{48,32},{1,49},{17,1},{33,17},{49,33},{2,50}... | collective-permute-start | bytes 5505032 | tf_op jit(solution)/shard_map/ppermute | solution.py:14
  13.4 166.9 %all-to-all-start = ((bf16[16,2,8,3584]{3,2,1,0:T(8,128)(2,1)}), bf16[16,2,8,3584]{3,2,1,0:T(8,128)(2,1)}, u32[]{:S(2)}, u32[]{:S(2)}) async-start(bf16[16,2,8,3584]{3,2,1,0:T(8,128)(2,1)} %pad_maximum_fusion.1), calls=%async_computation | async-start | bytes 3670016 | tf_op jit(solution)/shard_map/all_to_all | solution.py:94
  23.5 96.7 %collective-permute-start.4 = (bf16[256,3584]{1,0:T(8,128)(2,1)}, bf16[256,3584]{1,0:T(8,128)(2,1)S(1)}, u32[]{:S(2)}, u32[]{:S(2)}) collective-permute-start(bf16[256,3584]{1,0:T(8,128)(2,1)} %bitcast.142), channel_id=1, source_target_pairs={{0,16},{16,32},{32,48},{48,0},{1,17},{17,33},{33,49},{49,1},{2,18}... | collective-permute-start | bytes 5505032 | tf_op jit(solution)/shard_map/ppermute | solution.py:14
  41.7 81.7 %collective-permute-start.5 = (bf16[256,3584]{1,0:T(8,128)(2,1)}, bf16[256,3584]{1,0:T(8,128)(2,1)S(1)}, u32[]{:S(2)}, u32[]{:S(2)}) collective-permute-start(bf16[256,3584]{1,0:T(8,128)(2,1)} %bitcast.143), channel_id=1, source_target_pairs={{0,48},{16,0},{32,16},{48,32},{1,49},{17,1},{33,17},{49,33},{2,50}... | collective-permute-start | bytes 5505032 | tf_op jit(solution)/shard_map/ppermute | solution.py:14
  52.0 87.9 %collective-permute-start.6 = (bf16[3584,128]{1,0:T(8,128)(2,1)S(1)}, bf16[3584,128]{1,0:T(8,128)(2,1)S(1)}, u32[]{:S(2)}, u32[]{:S(2)}) collective-permute-start(bf16[3584,128]{1,0:T(8,128)(2,1)S(1)} %split.24), channel_id=1, source_target_pairs={{0,16},{16,32},{32,48},{48,0},{1,17},{17,33},{33,49},{49,1},{2,18}... | collective-permute-start | bytes 2752520 | tf_op jit(solution)/shard_map/ppermute | solution.py:14
  80.9 98.4 %collective-permute-start.7 = (bf16[3584,128]{1,0:T(8,128)(2,1)S(1)}, bf16[3584,128]{1,0:T(8,128)(2,1)S(1)}, u32[]{:S(2)}, u32[]{:S(2)}) collective-permute-start(bf16[3584,128]{1,0:T(8,128)(2,1)S(1)} %split.25), channel_id=1, source_target_pairs={{0,48},{16,0},{32,16},{48,32},{1,49},{17,1},{33,17},{49,33},{2,50}... | collective-permute-start | bytes 2752520 | tf_op jit(solution)/shard_map/ppermute | solution.py:14
  85.2 115.0 %collective-permute-start.8 = (bf16[3584,128]{1,0:T(8,128)(2,1)}, bf16[3584,128]{1,0:T(8,128)(2,1)}, u32[]{:S(2)}, u32[]{:S(2)}) collective-permute-start(bf16[3584,128]{1,0:T(8,128)(2,1)} %split.26), channel_id=1, source_target_pairs={{0,16},{16,32},{32,48},{48,0},{1,17},{17,33},{33,49},{49,1},{2,18}... | collective-permute-start | bytes 2752520 | tf_op jit(solution)/shard_map/ppermute | solution.py:14
  87.4 37.3 %copy-start.4 = (bf16[1,1,3584,256]{3,2,1,0:T(8,128)(2,1)S(1)}, bf16[1,1,3584,256]{3,2,1,0:T(8,128)(2,1)}, u32[]{:S(2)}) copy-start(bf16[1,1,3584,256]{3,2,1,0:T(8,128)(2,1)} %param.12) | copy-start | bytes 5505028
  120.2 3.2 copy-start.5
  120.2 82.2 %collective-permute-start.9 = (bf16[3584,128]{1,0:T(8,128)(2,1)}, bf16[3584,128]{1,0:T(8,128)(2,1)}, u32[]{:S(2)}, u32[]{:S(2)}) collective-permute-start(bf16[3584,128]{1,0:T(8,128)(2,1)} %split.27), channel_id=1, source_target_pairs={{0,48},{16,0},{32,16},{48,32},{1,49},{17,1},{33,17},{49,33},{2,50}... | collective-permute-start | bytes 2752520 | tf_op jit(solution)/shard_map/ppermute | solution.py:14
  123.4 2.8 copy-start.10
  123.4 55.8 %collective-permute-start.10 = (bf16[128,3584]{1,0:T(8,128)(2,1)S(1)}, bf16[128,3584]{1,0:T(8,128)(2,1)S(1)}, u32[]{:S(2)}, u32[]{:S(2)}) collective-permute-start(bf16[128,3584]{1,0:T(8,128)(2,1)S(1)} %split.28), channel_id=1, source_target_pairs={{0,16},{16,32},{32,48},{48,0},{1,17},{17,33},{33,49},{49,1},{2,18}... | collective-permute-start | bytes 2752520 | tf_op jit(solution)/shard_map/ppermute | solution.py:14
  139.9 64.7 %collective-permute-start.11 = (bf16[128,3584]{1,0:T(8,128)(2,1)}, bf16[128,3584]{1,0:T(8,128)(2,1)}, u32[]{:S(2)}, u32[]{:S(2)}) collective-permute-start(bf16[128,3584]{1,0:T(8,128)(2,1)} %split.29), channel_id=1, source_target_pairs={{0,48},{16,0},{32,16},{48,32},{1,49},{17,1},{33,17},{49,33},{2,50}... | collective-permute-start | bytes 2752520 | tf_op jit(solution)/shard_map/ppermute | solution.py:14
  180.3 6.2 %copy-start.6 = (bf16[256,3584]{1,0:T(8,128)(2,1)S(1)}, bf16[256,3584]{1,0:T(8,128)(2,1)}, u32[]{:S(2)}) copy-start(bf16[256,3584]{1,0:T(8,128)(2,1)} %copy-done.5) | copy-start | bytes 5505028
  180.3 6.2 %copy-start.11 = (bf16[256,3584]{1,0:T(8,128)(2,1)S(1)}, bf16[256,3584]{1,0:T(8,128)(2,1)}, u32[]{:S(2)}) copy-start(bf16[256,3584]{1,0:T(8,128)(2,1)} %copy-done.10) | copy-start | bytes 5505028
  180.3 6.2 %copy-start.15 = (bf16[1,1,256,3584]{3,2,1,0:T(8,128)(2,1)S(1)}, bf16[1,1,256,3584]{3,2,1,0:T(8,128)(2,1)}, u32[]{:S(2)}) copy-start(bf16[1,1,256,3584]{3,2,1,0:T(8,128)(2,1)} %param.13) | copy-start | bytes 5505028
  188.5 37.1 %all-to-all-start.1 = ((bf16[16,8,3584]{2,1,0:T(8,128)(2,1)}), bf16[16,8,3584]{2,1,0:T(8,128)(2,1)}, u32[]{:S(2)}, u32[]{:S(2)}) async-start(bf16[16,8,3584]{2,1,0:T(8,128)(2,1)} %fusion.12), calls=%async_computation.1 | async-start | bytes 1835008 | tf_op jit(solution)/shard_map/all_to_all | solution.py:72
  225.6 28.7 %all-to-all-start.2 = ((bf16[16,8,3584]{2,1,0:T(8,128)(2,1)}), bf16[16,8,3584]{2,1,0:T(8,128)(2,1)}, u32[]{:S(2)}, u32[]{:S(2)}) async-start(bf16[16,8,3584]{2,1,0:T(8,128)(2,1)} %fusion.13), calls=%async_computation.2 | async-start | bytes 1835008 | tf_op jit(solution)/shard_map/all_to_all | solution.py:72
  229.8 6.2 %copy-start.7 = (bf16[256,3584]{1,0:T(8,128)(2,1)S(1)}, bf16[256,3584]{1,0:T(8,128)(2,1)}, u32[]{:S(2)}) copy-start(bf16[256,3584]{1,0:T(8,128)(2,1)} %copy-done.5) | copy-start | bytes 5505028
  229.8 6.2 %copy-start.12 = (bf16[256,3584]{1,0:T(8,128)(2,1)S(1)}, bf16[256,3584]{1,0:T(8,128)(2,1)}, u32[]{:S(2)}) copy-start(bf16[256,3584]{1,0:T(8,128)(2,1)} %copy-done.10) | copy-start | bytes 5505028
  229.8 6.2 %copy-start.16 = (bf16[1,1,256,3584]{3,2,1,0:T(8,128)(2,1)S(1)}, bf16[1,1,256,3584]{3,2,1,0:T(8,128)(2,1)}, u32[]{:S(2)}) copy-start(bf16[1,1,256,3584]{3,2,1,0:T(8,128)(2,1)} %param.13) | copy-start | bytes 5505028
  254.2 28.7 %all-to-all-start.5 = ((bf16[16,8,3584]{2,1,0:T(8,128)(2,1)}), bf16[16,8,3584]{2,1,0:T(8,128)(2,1)}, u32[]{:S(2)}, u32[]{:S(2)}) async-start(bf16[16,8,3584]{2,1,0:T(8,128)(2,1)} %fusion.14), calls=%async_computation.5 | async-start | bytes 1835008 | tf_op jit(solution)/shard_map/all_to_all | solution.py:72
  283.0 28.7 %all-to-all-start.6 = ((bf16[16,8,3584]{2,1,0:T(8,128)(2,1)}), bf16[16,8,3584]{2,1,0:T(8,128)(2,1)}, u32[]{:S(2)}, u32[]{:S(2)}) async-start(bf16[16,8,3584]{2,1,0:T(8,128)(2,1)} %fusion.15), calls=%async_computation.6 | async-start | bytes 1835008 | tf_op jit(solution)/shard_map/all_to_all | solution.py:72
  289.4 13.6 %collective-permute-start.12 = (bf16[64,3584]{1,0:T(8,128)(2,1)S(1)}, bf16[64,3584]{1,0:T(8,128)(2,1)S(1)}, u32[]{:S(2)}, u32[]{:S(2)}) collective-permute-start(bf16[64,3584]{1,0:T(8,128)(2,1)S(1)} %fusion.16), channel_id=1, source_target_pairs={{0,64},{64,128},{128,192},{192,0},{1,65},{65,129},{129,193},{193,1... | collective-permute-start | bytes 1376264 | tf_op jit(solution)/shard_map/ppermute | solution.py:14
  311.7 28.7 %all-to-all-start.3 = ((bf16[16,8,3584]{2,1,0:T(8,128)(2,1)}), bf16[16,8,3584]{2,1,0:T(8,128)(2,1)S(1)}, u32[]{:S(2)}, u32[]{:S(2)}) async-start(bf16[16,8,3584]{2,1,0:T(8,128)(2,1)} %fusion.8), calls=%async_computation.3 | async-start | bytes 1835008 | tf_op jit(solution)/shard_map/all_to_all | solution.py:98
  318.6 13.5 %collective-permute-start.14 = (bf16[64,3584]{1,0:T(8,128)(2,1)S(1)}, bf16[64,3584]{1,0:T(8,128)(2,1)S(1)}, u32[]{:S(2)}, u32[]{:S(2)}) collective-permute-start(bf16[64,3584]{1,0:T(8,128)(2,1)S(1)} %fusion.17), channel_id=1, source_target_pairs={{0,64},{64,128},{128,192},{192,0},{1,65},{65,129},{129,193},{193,1... | collective-permute-start | bytes 1376264 | tf_op jit(solution)/shard_map/ppermute | solution.py:14
  332.0 0.8 copy-start.2
  340.4 28.7 %all-to-all-start.7 = ((bf16[16,8,3584]{2,1,0:T(8,128)(2,1)}), bf16[16,8,3584]{2,1,0:T(8,128)(2,1)}, u32[]{:S(2)}, u32[]{:S(2)}) async-start(bf16[16,8,3584]{2,1,0:T(8,128)(2,1)} %fusion.9), calls=%async_computation.7 | async-start | bytes 1835008 | tf_op jit(solution)/shard_map/all_to_all | solution.py:98
  347.9 5.9 %copy-start.8 = (bf16[256,3584]{1,0:T(8,128)(2,1)S(1)}, bf16[256,3584]{1,0:T(8,128)(2,1)}, u32[]{:S(2)}) copy-start(bf16[256,3584]{1,0:T(8,128)(2,1)} %copy-done.5) | copy-start | bytes 5505028
  347.9 5.9 %copy-start.13 = (bf16[256,3584]{1,0:T(8,128)(2,1)S(1)}, bf16[256,3584]{1,0:T(8,128)(2,1)}, u32[]{:S(2)}) copy-start(bf16[256,3584]{1,0:T(8,128)(2,1)} %copy-done.10) | copy-start | bytes 5505028
  347.9 5.9 %copy-start.17 = (bf16[1,1,256,3584]{3,2,1,0:T(8,128)(2,1)S(1)}, bf16[1,1,256,3584]{3,2,1,0:T(8,128)(2,1)}, u32[]{:S(2)}) copy-start(bf16[1,1,256,3584]{3,2,1,0:T(8,128)(2,1)} %param.13) | copy-start | bytes 5505028
  369.0 28.7 %all-to-all-start.4 = ((bf16[16,8,3584]{2,1,0:T(8,128)(2,1)}), bf16[16,8,3584]{2,1,0:T(8,128)(2,1)S(1)}, u32[]{:S(2)}, u32[]{:S(2)}) async-start(bf16[16,8,3584]{2,1,0:T(8,128)(2,1)} %fusion.11), calls=%async_computation.4 | async-start | bytes 1835008 | tf_op jit(solution)/shard_map/all_to_all | solution.py:72
  376.0 6.2 %copy-start.9 = (bf16[256,3584]{1,0:T(8,128)(2,1)S(1)}, bf16[256,3584]{1,0:T(8,128)(2,1)}, u32[]{:S(2)}) copy-start(bf16[256,3584]{1,0:T(8,128)(2,1)} %copy-done.5) | copy-start | bytes 5505028
  376.0 6.2 %copy-start.14 = (bf16[256,3584]{1,0:T(8,128)(2,1)S(1)}, bf16[256,3584]{1,0:T(8,128)(2,1)}, u32[]{:S(2)}) copy-start(bf16[256,3584]{1,0:T(8,128)(2,1)} %copy-done.10) | copy-start | bytes 5505028
  376.0 6.2 %copy-start.18 = (bf16[1,1,256,3584]{3,2,1,0:T(8,128)(2,1)S(1)}, bf16[1,1,256,3584]{3,2,1,0:T(8,128)(2,1)}, u32[]{:S(2)}) copy-start(bf16[1,1,256,3584]{3,2,1,0:T(8,128)(2,1)} %param.13) | copy-start | bytes 5505028
  384.1 17.4 %copy-start.3 = (bf16[64,3584]{1,0:T(8,128)(2,1)S(1)}, bf16[64,3584]{1,0:T(8,128)(2,1)}, u32[]{:S(2)}) copy-start(bf16[64,3584]{1,0:T(8,128)(2,1)} %copy-done.2) | copy-start | bytes 1376260
  397.7 28.6 %all-to-all-start.8 = ((bf16[16,8,3584]{2,1,0:T(8,128)(2,1)}), bf16[16,8,3584]{2,1,0:T(8,128)(2,1)S(1)}, u32[]{:S(2)}, u32[]{:S(2)}) async-start(bf16[16,8,3584]{2,1,0:T(8,128)(2,1)} %fusion.10), calls=%async_computation.8 | async-start | bytes 1835008 | tf_op jit(solution)/shard_map/all_to_all | solution.py:72
  403.0 24.9 %collective-permute-start.13 = (bf16[64,3584]{1,0:T(8,128)(2,1)}, bf16[64,3584]{1,0:T(8,128)(2,1)S(1)}, u32[]{:S(2)}, u32[]{:S(2)}) collective-permute-start(bf16[64,3584]{1,0:T(8,128)(2,1)} %fusion.18), channel_id=1, source_target_pairs={{0,64},{64,128},{128,192},{192,0},{1,65},{65,129},{129,193},{193,1... | collective-permute-start | bytes 1376264 | tf_op jit(solution)/shard_map/ppermute | solution.py:14
  426.6 12.1 %collective-permute-start.15 = (bf16[64,3584]{1,0:T(8,128)(2,1)S(1)}, bf16[64,3584]{1,0:T(8,128)(2,1)S(1)}, u32[]{:S(2)}, u32[]{:S(2)}) collective-permute-start(bf16[64,3584]{1,0:T(8,128)(2,1)S(1)} %fusion.19), channel_id=1, source_target_pairs={{0,64},{64,128},{128,192},{192,0},{1,65},{65,129},{129,193},{193,1... | collective-permute-start | bytes 1376264 | tf_op jit(solution)/shard_map/ppermute | solution.py:14
